TPU v7x, 256 devices: a whole 4x4x8 slice. The times are simulated.
256 devices in a mesh: dp: 16 (over z, core), tensor: 16 (over y, x).
Axes of the slice: x: 4, y: 4, z: 8, core: 2. Of those that a mesh axis runs over, the one named last changes fastest.
Arguments:
- tokens: bfloat16 [2048, 8192], P(('dp', 'tensor')), may hold values from -6 to 6
- hidden_grad: bfloat16 [2048, 14336], P('dp', 'tensor'), may hold values from -1.5 to 1.5
- gate_tiles: bfloat16 [16, 208, 128, 128], P('tensor', 'dp'), may hold values from -0.125 to 0.125
- up_tiles: bfloat16 [16, 208, 128, 128], P('tensor', 'dp'), may hold values from -0.125 to 0.125
- tile_rows: int32 [2, 112, 16], P(None, 'tensor'), may hold values from 0 to 63, all different within a row
- tile_owner: int32 [2, 112, 16], P(None, 'tensor'), may hold values from 0 to 15, as said below
Outputs:
- hidden: bfloat16 [2048, 14336], P('dp', 'tensor')
- token_grad: bfloat16 [2048, 8192], P(('dp', 'tensor'))
- gate_grad: bfloat16 [16, 208, 128, 128], P('tensor', 'dp')
- up_grad: bfloat16 [16, 208, 128, 128], P('tensor', 'dp')
Inputs may be any that keep to these rules, and one draw needn't show every extreme that they name: Each row tile_rows[m, f, :] names 16 different row blocks. For each m and t, among the 112 entries tile_owner[m, t * 7 .. (t + 1) * 7 - 1, :] no owner appears more than 13 times, and some owner appears exactly 13 times.
All inputs are finite; a program needn't handle non-finite values.
Results may differ from a plain program's by a relative error of at most 0.018.
Values may be sent and summed in bfloat16 or wider, within the bound.
No kernel may reach another device: no remote copies, remote signals or barrier semaphores. Data moves between devices by JAX's collectives and lax.ppermute only.
A program may use at most 128 MiB of HBM per device.

v0:
```python
import jax
import jax.numpy as jnp
from jax import lax
from jax.experimental import pallas as pl
from jax.experimental.pallas import tpu as pltpu
from jax.sharding import PartitionSpec as P


def slot_index(owner_ids, capacity):
    tile_total = owner_ids.shape[0]
    tile_order = jnp.arange(tile_total, dtype=jnp.int32)
    same_owner = (owner_ids[:, None] == owner_ids[None, :]) & (
        tile_order[None, :] < tile_order[:, None]
    )
    tile_ranks = jnp.sum(same_owner.astype(jnp.int32), axis=1)
    return owner_ids * capacity + tile_ranks


def _swiglu_kernel(rows_ref, slots_ref, tok_ref, tokt_ref, gstore_ref, ustore_ref, hgrad_ref,
                   hidden_ref, tpart_ref, grad_ref, acc_ref, delta_ref):
    group_blocks = hgrad_ref.shape[1] // 128
    per_block = rows_ref.shape[1] // group_blocks
    stores = (gstore_ref, ustore_ref)
    acc_ref[...] = jnp.zeros(acc_ref.shape, jnp.float32)
    grad_ref[...] = jnp.zeros(grad_ref.shape, grad_ref.dtype)
    for f in range(group_blocks):
        pre = []
        for m in range(2):
            def fwd_step(k, carry, m=m):
                i = f * per_block + k
                r = rows_ref[m, i]
                s = slots_ref[m, i]
                return carry + jnp.dot(tok_ref[r], stores[m][s], preferred_element_type=jnp.float32)
            pre.append(lax.fori_loop(0, per_block, fwd_step,
                                     jnp.zeros((128, 128), jnp.float32), unroll=True))
        gate_pre, up_pre = pre
        cols = slice(f * 128, (f + 1) * 128)
        hg = hgrad_ref[:, cols].astype(jnp.float32)
        sig = 1.0 / (1.0 + jnp.exp(-gate_pre))
        hidden_ref[:, cols] = (gate_pre * sig * up_pre).astype(hidden_ref.dtype)
        delta_ref[0] = (hg * up_pre * sig * (1.0 + gate_pre * (1.0 - sig))).astype(delta_ref.dtype)
        delta_ref[1] = (hg * gate_pre * sig).astype(delta_ref.dtype)

        def back_step(k, carry):
            i = f * per_block + k
            for m in range(2):
                r = rows_ref[m, i]
                s = slots_ref[m, i]
                d = delta_ref[m]
                back = lax.dot_general(d, stores[m][s], (((1,), (1,)), ((), ())),
                                       preferred_element_type=jnp.float32)
                acc_ref[r] = acc_ref[r] + back
                term = jnp.dot(tokt_ref[r], d, preferred_element_type=jnp.float32)
                grad_ref[s, m] = term.astype(grad_ref.dtype)
            return carry
        lax.fori_loop(0, per_block, back_step, 0, unroll=True)
    tpart_ref[...] = acc_ref[...].astype(tpart_ref.dtype)


def swiglu_local(rows, slots, tok_bm, tokt_bm, gstore, ustore, hgrad, interpret=False):
    row_blocks, tok_count, tile = tok_bm.shape
    slot_total = gstore.shape[0]
    smem = pl.BlockSpec(memory_space=pltpu.SMEM)
    vmem = pl.BlockSpec(memory_space=pltpu.VMEM)
    out_shape = (
        jax.ShapeDtypeStruct(hgrad.shape, jnp.bfloat16),
        jax.ShapeDtypeStruct((row_blocks, tok_count, tile), jnp.bfloat16),
        jax.ShapeDtypeStruct((slot_total, 2, tile, tile), jnp.bfloat16),
    )
    return pl.pallas_call(
        _swiglu_kernel,
        out_shape=out_shape,
        in_specs=[smem, smem, vmem, vmem, vmem, vmem, vmem],
        out_specs=(vmem, vmem, vmem),
        scratch_shapes=[pltpu.VMEM((row_blocks, tok_count, tile), jnp.float32),
                        pltpu.VMEM((2, tok_count, tile), jnp.bfloat16)],
        compiler_params=pltpu.CompilerParams(vmem_limit_bytes=100 * 1024 * 1024),
        interpret=interpret,
    )(rows, slots, tok_bm, tokt_bm, gstore, ustore, hgrad)


def body(tokens, hidden_grad, gate_tiles, up_tiles, tile_rows, tile_owner):
    tile_size = gate_tiles.shape[2]
    capacity = gate_tiles.shape[1]
    tensor_count = lax.axis_size("tensor")
    tok_copies = jnp.broadcast_to(tokens[None], (tensor_count,) + tokens.shape)
    gathered_tok = lax.all_to_all(tok_copies, "tensor", 0, 0, tiled=True).reshape(
        tensor_count * tokens.shape[0], tokens.shape[1]
    )
    tok_count, model_width = gathered_tok.shape
    row_blocks = model_width // tile_size
    tok_blocks = gathered_tok.reshape(tok_count, row_blocks, tile_size)
    tok_bm = tok_blocks.transpose(1, 0, 2)
    tokt_bm = tok_blocks.transpose(1, 2, 0)
    tile_count = tile_rows.shape[1] * tile_rows.shape[2]
    row_flat = tile_rows.reshape(2, tile_count)
    slot_stack = jnp.stack(
        [
            slot_index(tile_owner[0].reshape(-1), capacity),
            slot_index(tile_owner[1].reshape(-1), capacity),
        ],
        axis=0,
    )
    gate_store = lax.all_gather(gate_tiles[0], "dp", axis=0, tiled=True)
    up_store = lax.all_gather(up_tiles[0], "dp", axis=0, tiled=True)
    hidden, tpart_bm, grads = swiglu_local(
        row_flat, slot_stack, tok_bm, tokt_bm, gate_store, up_store, hidden_grad
    )
    token_part = tpart_bm.transpose(1, 0, 2).reshape(tok_count, model_width)
    part_rows = token_part.reshape(tensor_count, tok_count // tensor_count, model_width)
    part_recv = lax.all_to_all(part_rows, "tensor", 0, 0, tiled=True)
    token_grad = jnp.sum(part_recv.astype(jnp.float32), axis=0).astype(jnp.bfloat16)
    tile_sums = lax.psum_scatter(grads, "dp", scatter_dimension=0, tiled=True)
    gate_grad = tile_sums[:, 0][None]
    up_grad = tile_sums[:, 1][None]
    return (hidden, token_grad, gate_grad, up_grad)


def solution(mesh):
    placed = (
        P(("dp", "tensor"), None),
        P("dp", "tensor"),
        P("tensor", "dp", None, None),
        P("tensor", "dp", None, None),
        P(None, "tensor", None),
        P(None, "tensor", None),
    )
    return jax.shard_map(
        body,
        mesh=mesh,
        in_specs=placed,
        out_specs=(
            P("dp", "tensor"),
            P(("dp", "tensor"), None),
            P("tensor", "dp", None, None),
            P("tensor", "dp", None, None),
        ),
        check_vma=False,
    )
```

profile of v0, /device:TPU:2, one launch (start us, length us, event | category | flops | bytes accessed | tf_op | source)
XLA Modules:
  0.0 227.1 jit_solution(13706416537636293140)
XLA Ops:
  7.2 0.7 all-gather.5.cloned.1.call-update
  7.9 0.7 all-gather.7.cloned.1.call-update
  8.6 2.5 %broadcast_in_dim.2 = bf16[16,8,8192]{2,1,0:T(8,128)(2,1)} broadcast(bf16[8,8192]{1,0:T(8,128)(2,1)} %param.6), dimensions={1,2} | broadcast | bytes 2228224 | tf_op jit(solution)/shard_map/broadcast_in_dim | solution.py:86
  11.1 7.6 %all-to-all-start = ((bf16[16,8,8192]{2,1,0:T(8,128)(2,1)}), bf16[16,8,8192]{2,1,0:T(8,128)(2,1)S(1)}, u32[]{:S(2)}, u32[]{:S(2)}) async-start(bf16[16,8,8192]{2,1,0:T(8,128)(2,1)} %broadcast_in_dim.2), calls=%async_computation | async-start | bytes 4194304 | tf_op jit(solution)/shard_map/all_to_all | solution.py:87
  18.8 0.6 reshape.54.rows_ref
  19.5 0.1 eq.30
  19.6 0.1 eq.34
  19.8 0.2 convert_reduce_fusion.1
  20.0 0.2 convert_reduce_fusion
  20.2 0.6 pad_add_fusion.slots_ref
  20.7 25.1 %all-to-all-done = bf16[16,8,8192]{2,1,0:T(8,128)(2,1)S(1)} async-done(((bf16[16,8,8192]{2,1,0:T(8,128)(2,1)}), bf16[16,8,8192]{2,1,0:T(8,128)(2,1)S(1)}, u32[]{:S(2)}, u32[]{:S(2)}) %all-to-all-start) | async-done | bytes 2097184 | tf_op jit(solution)/shard_map/all_to_all | solution.py:87
  45.8 1.3 copy-done
  47.2 2.2 copy.29
  49.4 2.9 %copy.25 = bf16[128,64,128]{0,2,1:T(8,128)(2,1)} copy(bf16[128,64,128]{2,1,0:T(8,128)(2,1)S(1)} %bitcast.20) | data formatting | bytes 4194304 | tf_op jit(solution)/shard_map/reshape;reshape | solution.py:92
  52.4 2.7 %copy.31 = bf16[128,64,128]{2,0,1:T(8,128)(2,1)} copy(bf16[128,64,128]{2,1,0:T(8,128)(2,1)S(1)} %bitcast.21) | data formatting | bytes 4194304 | tf_op jit(solution)/shard_map/reshape;reshape | solution.py:92
  55.1 6.2 %all-gather.5.cloned.1.call-done = bf16[1,208,128,128]{3,2,0,1:T(8,128)(2,1)} async-done(((bf16[1,13,128,128]{3,2,0,1:T(8,128)(2,1)}), bf16[1,208,128,128]{3,2,0,1:T(8,128)(2,1)}) %all-gather.5.cloned.1.call-update) | async-done | bytes 6815760 | tf_op jit(solution)/shard_map/all_gather | solution.py:104
  61.2 48.9 %all-gather.7.cloned.1.call-done = bf16[1,208,128,128]{3,2,0,1:T(8,128)(2,1)} async-done(((bf16[1,13,128,128]{3,2,0,1:T(8,128)(2,1)}), bf16[1,208,128,128]{3,2,0,1:T(8,128)(2,1)}) %all-gather.7.cloned.1.call-update) | async-done | bytes 6815760 | tf_op jit(solution)/shard_map/all_gather | solution.py:105
  110.1 24.9 %shard_map.93 = (bf16[128,896]{1,0:T(8,128)(2,1)}, bf16[64,128,128]{2,1,0:T(8,128)(2,1)}, bf16[208,2,128,128]{3,2,1,0:T(8,128)(2,1)}) custom-call(s32[2,112]{1,0:T(2,128)} %reshape.54.rows_ref, s32[2,112]{1,0:T(2,128)} %pad_add_fusion.slots_ref, bf16[64,128,128]{2,1,0:T(8,128)(2,1)} %bitcast.23, bf16[64,128,128]{2,1,0:T(8,128)(2,1)} %bitcast.22, ...), custom_call_target="tpu_custom_call" | custom-call | tf_op jit(solution)/shard_map/pallas_call | solution.py:70
  135.0 2.9 %copy.28 = bf16[128,64,128]{2,1,0:T(8,128)(2,1)S(1)} copy(bf16[128,64,128]{2,0,1:T(8,128)(2,1)} %bitcast.27) | data formatting | bytes 4194304 | tf_op jit(solution)/shard_map/transpose | solution.py:109
  138.0 2.3 %reshape_reshape.7 = bf16[16,8,8192]{2,1,0:T(8,128)(2,1)} reshape(bf16[128,64,128]{2,1,0:T(8,128)(2,1)S(1)} %copy.28) | data formatting | bytes 4194304 | tf_op jit(solution)/shard_map/reshape;reshape | solution.py:110
  140.3 34.7 %all_to_all.10 = bf16[16,8,8192]{2,1,0:T(8,128)(2,1)S(1)} all-to-all(bf16[16,8,8192]{2,1,0:T(8,128)(2,1)} %reshape_reshape.7), channel_id=1, replica_groups=mesh['dp'=16,'tensor'=16] {'tensor'}, dimensions={0} | all-to-all | bytes 4194304 | tf_op jit(solution)/shard_map/all_to_all | solution.py:111
  175.0 1.0 reduce_sum.38
  175.9 42.5 %reduce-scatter.2.cloned.1.call-done = bf16[13,2,128,128]{3,2,1,0:T(8,128)(2,1)} async-done(((bf16[208,2,128,128]{3,2,1,0:T(8,128)(2,1)}), bf16[13,2,128,128]{3,2,1,0:T(8,128)(2,1)}) %reduce-scatter.2.cloned.1.call-update) | async-done | bytes 851984 | tf_op jit(solution)/shard_map/reduce_scatter | solution.py:113
  218.4 2.1 slice_bitcast_fusion
  (14 shorter events, 0.3 us)
Async XLA Ops:
  7.2 54.1 %all-gather.5.cloned.1.call-start = ((), (), s32[]{:S(2)}) async-start(), calls=%async_computation.4 | async-start | bytes 7241728 | tf_op jit(solution)/shard_map/all_gather | solution.py:104
  7.9 102.2 %all-gather.7.cloned.1.call-start = ((), (), s32[]{:S(2)}) async-start(), calls=%async_computation.5 | async-start | bytes 7241728 | tf_op jit(solution)/shard_map/all_gather | solution.py:105
  11.1 7.7 %copy-start.1 = (s32[2,7,16]{2,0,1:T(2,128)S(1)}, s32[2,7,16]{2,0,1:T(2,128)}, u32[]{:S(2)}) copy-start(s32[2,7,16]{2,0,1:T(2,128)} %param.10) | copy-start | bytes 2692
  11.1 8.3 %copy-start.2 = (s32[2,7,16]{2,0,1:T(2,128)S(1)}, s32[2,7,16]{2,0,1:T(2,128)}, u32[]{:S(2)}) copy-start(s32[2,7,16]{2,0,1:T(2,128)} %param.11) | copy-start | bytes 2692
  11.1 34.7 %all-to-all-start = ((bf16[16,8,8192]{2,1,0:T(8,128)(2,1)}), bf16[16,8,8192]{2,1,0:T(8,128)(2,1)S(1)}, u32[]{:S(2)}, u32[]{:S(2)}) async-start(bf16[16,8,8192]{2,1,0:T(8,128)(2,1)} %broadcast_in_dim.2), calls=%async_computation | async-start | bytes 4194304 | tf_op jit(solution)/shard_map/all_to_all | solution.py:87
  18.7 199.7 %reduce-scatter.2.cloned.1.call-start = ((), (), s32[]{:S(2)}) async-start(), calls=%async_computation.3 | async-start | bytes 14483456 | tf_op jit(solution)/shard_map/reduce_scatter | solution.py:113
  45.8 1.4 copy-start
Sparse Core Ops, SparseCore 0:
  9.8 51.3 all-gather.4
  63.1 46.9 all-gather.6
  135.1 83.2 reduce-scatter.1
where the time goes:
time: 227 us
  waiting for transfers between devices  124 us (55%)
  blocking collectives  34.7 us (15%)
  Pallas kernels  24.9 us (11%)
  local copies, waits for them, and re-layouts  20 us (9%)
  between operations  13.8 us (6%)
  starting transfers between devices  7.72 us (3%)
    all_gather x1, waiting for transfers between devices, body(): up_store = lax.all_gather(up_tiles[0], 'dp', axis=0, tiled=True)  48.9 us
    reduce_scatter x1, waiting for transfers between devices, body(): tile_sums = lax.psum_scatter(grads, 'dp', scatter_dimension=0, tiled=True)  42.5 us
    all_to_all x1, blocking collectives, body(): part_recv = lax.all_to_all(part_rows, 'tensor', 0, 0, tiled=True)  34.7 us
    all_to_all x1, waiting for transfers between devices, body(): lax.all_to_all(tok_copies, 'tensor', 0, 0, tiled=True)  25.1 us
    pallas_call x1, Pallas kernels, swiglu_local(): pl.pallas_call(_swiglu_kernel, out_shape=out_shape, in_specs=[smem, smem,...  24.9 us
    all_to_all x1, starting transfers between devices, body(): lax.all_to_all(tok_copies, 'tensor', 0, 0, tiled=True)  7.61 us
    all_gather x1, waiting for transfers between devices, body(): gate_store = lax.all_gather(gate_tiles[0], 'dp', axis=0, tiled=True)  6.16 us
    another operation x2, local copies, waits for them, and re-layouts, body(): tok_blocks = gathered_tok.reshape(tok_count, row_blocks, tile_size)  5.64 us
  transfers between devices with their start and end apart: 4, of which 4 were waited for; matrix products, arithmetic and copies ran while one was open for 8% of the time, Pallas kernels for 0%

commit v1 on v0

--- a/solution.py
+++ b/solution.py
@@ -6,14 +6,16 @@
 from jax.sharding import PartitionSpec as P
 
 
-def slot_index(owner_ids, capacity):
+def slot_index(owner_ids, capacity, core_count, chip_count):
     tile_total = owner_ids.shape[0]
     tile_order = jnp.arange(tile_total, dtype=jnp.int32)
     same_owner = (owner_ids[:, None] == owner_ids[None, :]) & (
         tile_order[None, :] < tile_order[:, None]
     )
     tile_ranks = jnp.sum(same_owner.astype(jnp.int32), axis=1)
-    return owner_ids * capacity + tile_ranks
+    owner_core = owner_ids % core_count
+    owner_chip = owner_ids // core_count
+    return (owner_core * chip_count + owner_chip) * capacity + tile_ranks
 
 
 def _swiglu_kernel(rows_ref, slots_ref, tok_ref, tokt_ref, gstore_ref, ustore_ref, hgrad_ref,
@@ -94,15 +96,21 @@
     tokt_bm = tok_blocks.transpose(1, 2, 0)
     tile_count = tile_rows.shape[1] * tile_rows.shape[2]
     row_flat = tile_rows.reshape(2, tile_count)
+    core_count = lax.axis_size("core")
+    chip_count = lax.axis_size("z")
     slot_stack = jnp.stack(
         [
-            slot_index(tile_owner[0].reshape(-1), capacity),
-            slot_index(tile_owner[1].reshape(-1), capacity),
+            slot_index(tile_owner[0].reshape(-1), capacity, core_count, chip_count),
+            slot_index(tile_owner[1].reshape(-1), capacity, core_count, chip_count),
         ],
         axis=0,
     )
-    gate_store = lax.all_gather(gate_tiles[0], "dp", axis=0, tiled=True)
-    up_store = lax.all_gather(up_tiles[0], "dp", axis=0, tiled=True)
+    gate_store = lax.all_gather(
+        lax.all_gather(gate_tiles[0], "z", axis=0, tiled=True), "core", axis=0, tiled=True
+    )
+    up_store = lax.all_gather(
+        lax.all_gather(up_tiles[0], "z", axis=0, tiled=True), "core", axis=0, tiled=True
+    )
     hidden, tpart_bm, grads = swiglu_local(
         row_flat, slot_stack, tok_bm, tokt_bm, gate_store, up_store, hidden_grad
     )
@@ -110,30 +118,37 @@
     part_rows = token_part.reshape(tensor_count, tok_count // tensor_count, model_width)
     part_recv = lax.all_to_all(part_rows, "tensor", 0, 0, tiled=True)
     token_grad = jnp.sum(part_recv.astype(jnp.float32), axis=0).astype(jnp.bfloat16)
-    tile_sums = lax.psum_scatter(grads, "dp", scatter_dimension=0, tiled=True)
+    core_sums = lax.psum_scatter(grads, "core", scatter_dimension=0, tiled=True)
+    tile_sums = lax.psum_scatter(core_sums, "z", scatter_dimension=0, tiled=True)
     gate_grad = tile_sums[:, 0][None]
     up_grad = tile_sums[:, 1][None]
     return (hidden, token_grad, gate_grad, up_grad)
 
 
 def solution(mesh):
+    dp_size = mesh.shape["dp"]
+    chip_count = dp_size // 2
+    split_mesh = jax.sharding.Mesh(
+        mesh.devices.reshape(chip_count, 2, mesh.shape["tensor"]), ("z", "core", "tensor")
+    )
+    dp = ("z", "core")
     placed = (
-        P(("dp", "tensor"), None),
-        P("dp", "tensor"),
-        P("tensor", "dp", None, None),
-        P("tensor", "dp", None, None),
+        P(dp + ("tensor",), None),
+        P(dp, "tensor"),
+        P("tensor", dp, None, None),
+        P("tensor", dp, None, None),
         P(None, "tensor", None),
         P(None, "tensor", None),
     )
     return jax.shard_map(
         body,
-        mesh=mesh,
+        mesh=split_mesh,
         in_specs=placed,
         out_specs=(
-            P("dp", "tensor"),
-            P(("dp", "tensor"), None),
-            P("tensor", "dp", None, None),
-            P("tensor", "dp", None, None),
+            P(dp, "tensor"),
+            P(dp + ("tensor",), None),
+            P("tensor", dp, None, None),
+            P("tensor", dp, None, None),
         ),
         check_vma=False,
     )

time: 227 us -> 306 us (1.35)
  waiting for transfers between devices: 124 us -> 203 us
    all_gather x2 -> x4, waiting for transfers between devices: 55 us -> 103 us  [the longest x1 51.4 us: body(): lax.all_gather(gate_tiles[0], 'z', axis=0, tiled=True)]
    reduce_scatter x1 -> x2, waiting for transfers between devices: 42.5 us -> 74.2 us  [the longest x1 44.2 us: body(): lax.psum_scatter(core_sums, 'z', scatter_dimension=0, tiled=True)]
  transfers between devices with their start and end apart: 4 -> 7, of which waited for: 4 -> 6; matrix products, arithmetic and copies ran while one was open for 8% -> 6% of each run, Pallas kernels for 0% -> 0%
where the time goes in v1:
time: 306 us; the launch traced here: 305 us
  waiting for transfers between devices  203 us (66%)
  blocking collectives  33.4 us (11%)
  Pallas kernels  24.9 us (8%)
  local copies, waits for them, and re-layouts  19.5 us (6%)
  between operations  14.2 us (5%)
  starting transfers between devices  7.81 us (3%)
    all_gather x1, waiting for transfers between devices, body(): lax.all_gather(gate_tiles[0], 'z', axis=0, tiled=True)  51.4 us
    all_gather x1, waiting for transfers between devices, body(): lax.all_gather(up_tiles[0], 'z', axis=0, tiled=True)  47.7 us
    reduce_scatter x1, waiting for transfers between devices, body(): lax.psum_scatter(core_sums, 'z', scatter_dimension=0, tiled=True)  44.2 us
    all_to_all x1, blocking collectives, body(): part_recv = lax.all_to_all(part_rows, 'tensor', 0, 0, tiled=True)  33.4 us
    reduce_scatter x1, waiting for transfers between devices, body(): core_sums = lax.psum_scatter(grads, 'core', scatter_dimension=0, tiled=True)  30 us
    all_to_all x1, waiting for transfers between devices, body(): lax.all_to_all(tok_copies, 'tensor', 0, 0, tiled=True)  24.9 us
    pallas_call x1, Pallas kernels, swiglu_local(): pl.pallas_call(_swiglu_kernel, out_shape=out_shape, in_specs=[smem, smem,...  24.9 us
    all_to_all x1, starting transfers between devices, body(): lax.all_to_all(tok_copies, 'tensor', 0, 0, tiled=True)  7.4 us
  transfers between devices with their start and end apart: 7, of which 6 were waited for; matrix products, arithmetic and copies ran while one was open for 6% of the time, Pallas kernels for 0%

profile of v1, /device:TPU:2, one launch (start us, length us, event | category | flops | bytes accessed | tf_op | source)
XLA Modules:
  0.0 305.0 jit_solution(9664455521303018961)
XLA Ops:
  7.2 0.7 all-gather.9.cloned.1.call-update
  7.9 0.7 all-gather.13.cloned.1.call-update
  8.7 51.4 %all-gather.9.cloned.1.call-done = bf16[1,104,128,128]{3,2,0,1:T(8,128)(2,1)} async-done(((bf16[1,13,128,128]{3,2,0,1:T(8,128)(2,1)}), bf16[1,104,128,128]{3,2,0,1:T(8,128)(2,1)}) %all-gather.9.cloned.1.call-update) | async-done | bytes 3407888 | tf_op jit(solution)/shard_map/all_gather | solution.py:109
  60.2 47.7 %all-gather.13.cloned.1.call-done = bf16[1,104,128,128]{3,2,0,1:T(8,128)(2,1)} async-done(((bf16[1,13,128,128]{3,2,0,1:T(8,128)(2,1)}), bf16[1,104,128,128]{3,2,0,1:T(8,128)(2,1)}) %all-gather.13.cloned.1.call-update) | async-done | bytes 3407888 | tf_op jit(solution)/shard_map/all_gather | solution.py:112
  108.0 1.6 broadcast_in_dim.2
  109.6 7.4 %all-to-all-start = ((bf16[16,8,8192]{2,1,0:T(8,128)(2,1)}), bf16[16,8,8192]{2,1,0:T(8,128)(2,1)S(1)}, u32[]{:S(2)}, u32[]{:S(2)}) async-start(bf16[16,8,8192]{2,1,0:T(8,128)(2,1)} %broadcast_in_dim.2), calls=%async_computation | async-start | bytes 4194304 | tf_op jit(solution)/shard_map/all_to_all | solution.py:89
  117.4 0.6 reshape.238.rows_ref
  118.2 0.2 convert_reduce_fusion
  118.4 0.6 pad_add_fusion.slots_ref
  119.0 24.9 %all-to-all-done = bf16[16,8,8192]{2,1,0:T(8,128)(2,1)S(1)} async-done(((bf16[16,8,8192]{2,1,0:T(8,128)(2,1)}), bf16[16,8,8192]{2,1,0:T(8,128)(2,1)S(1)}, u32[]{:S(2)}, u32[]{:S(2)}) %all-to-all-start) | async-done | bytes 2097184 | tf_op jit(solution)/shard_map/all_to_all | solution.py:89
  143.9 1.4 copy-done
  145.3 2.5 copy.29
  147.8 3.0 copy.25
  150.8 2.7 copy.31
  153.5 3.6 %all-gather.15.cloned.1.call-done = bf16[1,208,128,128]{3,2,0,1:T(8,128)(2,1)} async-done(((bf16[1,104,128,128]{3,2,0,1:T(8,128)(2,1)}), bf16[1,208,128,128]{3,2,0,1:T(8,128)(2,1)}) %all-gather.15.cloned.1.call-update) | async-done | bytes 6815760 | tf_op jit(solution)/shard_map/all_gather | solution.py:111
  157.1 24.9 %shard_map.93 = (bf16[128,896]{1,0:T(8,128)(2,1)}, bf16[64,128,128]{2,1,0:T(8,128)(2,1)}, bf16[208,2,128,128]{3,2,1,0:T(8,128)(2,1)}) custom-call(s32[2,112]{1,0:T(2,128)} %reshape.238.rows_ref, s32[2,112]{1,0:T(2,128)} %pad_add_fusion.slots_ref, bf16[64,128,128]{2,1,0:T(8,128)(2,1)} %bitcast.23, bf16[64,128,128]{2,1,0:T(8,128)(2,1)} %bitcast.22, ...), custom_call_target="tpu_custom_call" | custom-call | tf_op jit(solution)/shard_map/pallas_call | solution.py:72
  182.0 0.2 reduce-scatter.5.cloned.1.call-start
  182.2 30.0 %reduce-scatter.3.cloned.1.call-done = bf16[104,2,128,128]{3,2,1,0:T(8,128)(2,1)} async-done(((bf16[208,2,128,128]{3,2,1,0:T(8,128)(2,1)}), bf16[104,2,128,128]{3,2,1,0:T(8,128)(2,1)}) %reduce-scatter.3.cloned.1.call-update) | async-done | bytes 6815760 | tf_op jit(solution)/shard_map/reduce_scatter | solution.py:121
  212.2 2.9 copy.28
  215.2 2.3 reshape_reshape.7
  217.5 33.4 %all_to_all.10 = bf16[16,8,8192]{2,1,0:T(8,128)(2,1)S(1)} all-to-all(bf16[16,8,8192]{2,1,0:T(8,128)(2,1)} %reshape_reshape.7), channel_id=1, replica_groups=mesh['z'=8,'core'=2,'tensor'=16] {'tensor'}, dimensions={0} | all-to-all | bytes 4194304 | tf_op jit(solution)/shard_map/all_to_all | solution.py:119
  250.8 1.0 reduce_sum.38
  251.8 44.2 %reduce-scatter.5.cloned.1.call-done = bf16[13,2,128,128]{3,2,1,0:T(8,128)(2,1)} async-done(((bf16[104,2,128,128]{3,2,1,0:T(8,128)(2,1)}), bf16[13,2,128,128]{3,2,1,0:T(8,128)(2,1)}) %reduce-scatter.5.cloned.1.call-update) | async-done | bytes 851984 | tf_op jit(solution)/shard_map/reduce_scatter | solution.py:122
  296.0 2.1 slice_bitcast_fusion
  (25 shorter events, 0.8 us)
Async XLA Ops:
  7.2 53.0 %all-gather.9.cloned.1.call-start = ((), (), s32[]{:S(2)}) async-start(), calls=%async_computation.6 | async-start | bytes 3833856 | tf_op jit(solution)/shard_map/all_gather | solution.py:109
  7.9 100.0 %all-gather.13.cloned.1.call-start = ((), (), s32[]{:S(2)}) async-start(), calls=%async_computation.8 | async-start | bytes 3833856 | tf_op jit(solution)/shard_map/all_gather | solution.py:112
  8.6 144.8 %all-gather.11.cloned.1.call-start = ((), (), s32[]{:S(2)}) async-start(), calls=%async_computation.7 | async-start | bytes 10223616 | tf_op jit(solution)/shard_map/all_gather | solution.py:108
  60.1 47.8 %copy-start.1 = (bf16[8,8192]{1,0:T(8,128)(2,1)S(1)}, bf16[8,8192]{1,0:T(8,128)(2,1)}, u32[]{:S(2)}) copy-start(bf16[8,8192]{1,0:T(8,128)(2,1)} %param.6) | copy-start | bytes 393220
  60.2 96.9 %all-gather.15.cloned.1.call-start = ((), (), s32[]{:S(2)}) async-start(), calls=%async_computation.9 | async-start | bytes 10223616 | tf_op jit(solution)/shard_map/all_gather | solution.py:111
  109.6 7.5 %copy-start.2 = (s32[2,7,16]{2,0,1:T(2,128)S(1)}, s32[2,7,16]{2,0,1:T(2,128)}, u32[]{:S(2)}) copy-start(s32[2,7,16]{2,0,1:T(2,128)} %param.11) | copy-start | bytes 2692
  109.6 7.8 %copy-start.3 = (s32[2,7,16]{2,0,1:T(2,128)S(1)}, s32[2,7,16]{2,0,1:T(2,128)}, u32[]{:S(2)}) copy-start(s32[2,7,16]{2,0,1:T(2,128)} %param.10) | copy-start | bytes 2692
  109.6 34.4 %all-to-all-start = ((bf16[16,8,8192]{2,1,0:T(8,128)(2,1)}), bf16[16,8,8192]{2,1,0:T(8,128)(2,1)S(1)}, u32[]{:S(2)}, u32[]{:S(2)}) async-start(bf16[16,8,8192]{2,1,0:T(8,128)(2,1)} %broadcast_in_dim.2), calls=%async_computation | async-start | bytes 4194304 | tf_op jit(solution)/shard_map/all_to_all | solution.py:89
  117.0 95.2 %reduce-scatter.3.cloned.1.call-start = ((), (), s32[]{:S(2)}) async-start(), calls=%async_computation.4 | async-start | bytes 20447232 | tf_op jit(solution)/shard_map/reduce_scatter | solution.py:121
  143.9 1.4 copy-start
  182.0 114.0 %reduce-scatter.5.cloned.1.call-start = ((), (), s32[]{:S(2)}) async-start(), calls=%async_computation.5 | async-start | bytes 7667712 | tf_op jit(solution)/shard_map/reduce_scatter | solution.py:122
Sparse Core Ops, SparseCore 0:
  9.8 50.3 all-gather.8
  61.9 45.9 all-gather.12
  109.7 21.4 all-gather.10
  132.9 24.1 all-gather.14
  182.1 30.0 reduce-scatter.2
  214.6 81.3 reduce-scatter.4

commit v2 on v0

--- a/solution.py
+++ b/solution.py
@@ -16,11 +16,10 @@
     return owner_ids * capacity + tile_ranks
 
 
-def _swiglu_kernel(rows_ref, slots_ref, tok_ref, tokt_ref, gstore_ref, ustore_ref, hgrad_ref,
+def _swiglu_kernel(rows_ref, slots_ref, tok_ref, tokt_ref, store_ref, hgrad_ref,
                    hidden_ref, tpart_ref, grad_ref, acc_ref, delta_ref):
     group_blocks = hgrad_ref.shape[1] // 128
     per_block = rows_ref.shape[1] // group_blocks
-    stores = (gstore_ref, ustore_ref)
     acc_ref[...] = jnp.zeros(acc_ref.shape, jnp.float32)
     grad_ref[...] = jnp.zeros(grad_ref.shape, grad_ref.dtype)
     for f in range(group_blocks):
@@ -30,7 +29,7 @@
                 i = f * per_block + k
                 r = rows_ref[m, i]
                 s = slots_ref[m, i]
-                return carry + jnp.dot(tok_ref[r], stores[m][s], preferred_element_type=jnp.float32)
+                return carry + jnp.dot(tok_ref[r], store_ref[s, m], preferred_element_type=jnp.float32)
             pre.append(lax.fori_loop(0, per_block, fwd_step,
                                      jnp.zeros((128, 128), jnp.float32), unroll=True))
         gate_pre, up_pre = pre
@@ -47,7 +46,7 @@
                 r = rows_ref[m, i]
                 s = slots_ref[m, i]
                 d = delta_ref[m]
-                back = lax.dot_general(d, stores[m][s], (((1,), (1,)), ((), ())),
+                back = lax.dot_general(d, store_ref[s, m], (((1,), (1,)), ((), ())),
                                        preferred_element_type=jnp.float32)
                 acc_ref[r] = acc_ref[r] + back
                 term = jnp.dot(tokt_ref[r], d, preferred_element_type=jnp.float32)
@@ -57,9 +56,9 @@
     tpart_ref[...] = acc_ref[...].astype(tpart_ref.dtype)
 
 
-def swiglu_local(rows, slots, tok_bm, tokt_bm, gstore, ustore, hgrad, interpret=False):
+def swiglu_local(rows, slots, tok_bm, tokt_bm, store, hgrad, interpret=False):
     row_blocks, tok_count, tile = tok_bm.shape
-    slot_total = gstore.shape[0]
+    slot_total = store.shape[0]
     smem = pl.BlockSpec(memory_space=pltpu.SMEM)
     vmem = pl.BlockSpec(memory_space=pltpu.VMEM)
     out_shape = (
@@ -70,13 +69,13 @@
     return pl.pallas_call(
         _swiglu_kernel,
         out_shape=out_shape,
-        in_specs=[smem, smem, vmem, vmem, vmem, vmem, vmem],
+        in_specs=[smem, smem, vmem, vmem, vmem, vmem],
         out_specs=(vmem, vmem, vmem),
         scratch_shapes=[pltpu.VMEM((row_blocks, tok_count, tile), jnp.float32),
                         pltpu.VMEM((2, tok_count, tile), jnp.bfloat16)],
         compiler_params=pltpu.CompilerParams(vmem_limit_bytes=100 * 1024 * 1024),
         interpret=interpret,
-    )(rows, slots, tok_bm, tokt_bm, gstore, ustore, hgrad)
+    )(rows, slots, tok_bm, tokt_bm, store, hgrad)
 
 
 def body(tokens, hidden_grad, gate_tiles, up_tiles, tile_rows, tile_owner):
@@ -101,10 +100,10 @@
         ],
         axis=0,
     )
-    gate_store = lax.all_gather(gate_tiles[0], "dp", axis=0, tiled=True)
-    up_store = lax.all_gather(up_tiles[0], "dp", axis=0, tiled=True)
+    local_pair = jnp.stack([gate_tiles[0], up_tiles[0]], axis=1)
+    store = lax.all_gather(local_pair, "dp", axis=0, tiled=True)
     hidden, tpart_bm, grads = swiglu_local(
-        row_flat, slot_stack, tok_bm, tokt_bm, gate_store, up_store, hidden_grad
+        row_flat, slot_stack, tok_bm, tokt_bm, store, hidden_grad
     )
     token_part = tpart_bm.transpose(1, 0, 2).reshape(tok_count, model_width)
     part_rows = token_part.reshape(tensor_count, tok_count // tensor_count, model_width)

time: 227 us -> 211 us (0.930)
  waiting for transfers between devices: 124 us -> 106 us
    all_gather x2 -> x1, waiting for transfers between devices: 55 us -> 38.5 us  [body(): store = lax.all_gather(local_pair, 'dp', axis=0, tiled=True)]
  transfers between devices with their start and end apart: 4 -> 3, of which waited for: 4 -> 3; matrix products, arithmetic and copies ran while one was open for 8% -> 8% of each run, Pallas kernels for 0% -> 0%
where the time goes in v2:
time: 211 us
  waiting for transfers between devices  106 us (50%)
  blocking collectives  34.7 us (16%)
  Pallas kernels  24.9 us (12%)
  local copies, waits for them, and re-layouts  19 us (9%)
  between operations  14.1 us (7%)
  starting transfers between devices  7.68 us (4%)
  other arithmetic  4.12 us (2%)
    reduce_scatter x1, waiting for transfers between devices, body(): tile_sums = lax.psum_scatter(grads, 'dp', scatter_dimension=0, tiled=True)  42.5 us
    all_gather x1, waiting for transfers between devices, body(): store = lax.all_gather(local_pair, 'dp', axis=0, tiled=True)  38.5 us
    all_to_all x1, blocking collectives, body(): part_recv = lax.all_to_all(part_rows, 'tensor', 0, 0, tiled=True)  34.7 us
    all_to_all x1, waiting for transfers between devices, body(): lax.all_to_all(tok_copies, 'tensor', 0, 0, tiled=True)  25.1 us
    pallas_call x1, Pallas kernels, swiglu_local(): pl.pallas_call(_swiglu_kernel, out_shape=out_shape, in_specs=[smem, smem,...  24.9 us
    all_to_all x1, starting transfers between devices, body(): lax.all_to_all(tok_copies, 'tensor', 0, 0, tiled=True)  7.61 us
    another operation x2, local copies, waits for them, and re-layouts, body(): tok_blocks = gathered_tok.reshape(tok_count, row_blocks, tile_size)  5.61 us
  transfers between devices with their start and end apart: 3, of which 3 were waited for; matrix products, arithmetic and copies ran while one was open for 8% of the time, Pallas kernels for 0%

profile of v2, /device:TPU:2, one launch (start us, length us, event | category | flops | bytes accessed | tf_op | source)
XLA Modules:
  0.0 210.7 jit_solution(2871059983350054094)
XLA Ops:
  7.2 2.2 %pad_maximum_fusion = bf16[13,2,128,128]{3,2,1,0:T(8,128)(2,1)} fusion(bf16[13,1,128,128]{3,2,1,0:T(8,128)(2,1)} %bitcast.24, bf16[13,1,128,128]{3,2,1,0:T(8,128)(2,1)} %bitcast.25), kind=kLoop, calls=%fused_computation.1 | loop fusion | flops 425984 | bytes 1703936 | tf_op jit(solution)/shard_map/stack | solution.py:103
  9.4 1.5 broadcast_in_dim.2
  10.9 7.6 %all-to-all-start = ((bf16[16,8,8192]{2,1,0:T(8,128)(2,1)}), bf16[16,8,8192]{2,1,0:T(8,128)(2,1)S(1)}, u32[]{:S(2)}, u32[]{:S(2)}) async-start(bf16[16,8,8192]{2,1,0:T(8,128)(2,1)} %broadcast_in_dim.2), calls=%async_computation | async-start | bytes 4194304 | tf_op jit(solution)/shard_map/all_to_all | solution.py:86
  18.6 0.6 reshape.54.rows_ref
  19.3 0.1 eq.30
  19.4 0.1 eq.34
  19.5 0.1 mul.29
  19.5 0.1 mul.27
  19.6 0.2 convert_reduce_fusion.1
  19.8 0.2 convert_reduce_fusion
  20.0 0.6 pad_add_fusion.slots_ref
  20.6 25.1 %all-to-all-done = bf16[16,8,8192]{2,1,0:T(8,128)(2,1)S(1)} async-done(((bf16[16,8,8192]{2,1,0:T(8,128)(2,1)}), bf16[16,8,8192]{2,1,0:T(8,128)(2,1)S(1)}, u32[]{:S(2)}, u32[]{:S(2)}) %all-to-all-start) | async-done | bytes 2097184 | tf_op jit(solution)/shard_map/all_to_all | solution.py:86
  45.7 1.3 copy-done
  47.0 2.2 %copy.25 = bf16[16,8,64,128]{3,2,1,0:T(8,128)(2,1)S(1)} copy(bf16[16,8,64,128]{3,1,2,0:T(8,128)(2,1)} %bitcast.22) | data formatting | bytes 4194304
  49.2 3.0 %copy.23 = bf16[128,64,128]{0,2,1:T(8,128)(2,1)} copy(bf16[128,64,128]{2,1,0:T(8,128)(2,1)S(1)} %bitcast.18) | data formatting | bytes 4194304 | tf_op jit(solution)/shard_map/reshape;reshape | solution.py:91
  52.2 2.6 %copy.27 = bf16[128,64,128]{2,0,1:T(8,128)(2,1)} copy(bf16[128,64,128]{2,1,0:T(8,128)(2,1)S(1)} %bitcast.19) | data formatting | bytes 4194304 | tf_op jit(solution)/shard_map/reshape;reshape | solution.py:91
  54.8 38.5 %all-gather.2.cloned.1.call-done.store_ref = bf16[208,2,128,128]{3,2,1,0:T(8,128)(2,1)} async-done(((bf16[13,2,128,128]{3,2,1,0:T(8,128)(2,1)}), bf16[208,2,128,128]{3,2,1,0:T(8,128)(2,1)}) %all-gather.2.cloned.1.call-update) | async-done | bytes 13631504 | tf_op jit(solution)/shard_map/all_gather | solution.py:104
  93.3 24.9 %shard_map.93 = (bf16[128,896]{1,0:T(8,128)(2,1)}, bf16[64,128,128]{2,1,0:T(8,128)(2,1)}, bf16[208,2,128,128]{3,2,1,0:T(8,128)(2,1)}) custom-call(s32[2,112]{1,0:T(2,128)} %reshape.54.rows_ref, s32[2,112]{1,0:T(2,128)} %pad_add_fusion.slots_ref, bf16[64,128,128]{2,1,0:T(8,128)(2,1)} %bitcast.21, bf16[64,128,128]{2,1,0:T(8,128)(2,1)} %bitcast.20, ...), custom_call_target="tpu_custom_call" | custom-call | tf_op jit(solution)/shard_map/pallas_call | solution.py:69
  118.3 2.9 %copy.24 = bf16[128,64,128]{2,1,0:T(8,128)(2,1)S(1)} copy(bf16[128,64,128]{2,0,1:T(8,128)(2,1)} %bitcast.23) | data formatting | bytes 4194304 | tf_op jit(solution)/shard_map/transpose | solution.py:108
  121.2 2.3 %reshape_reshape.7 = bf16[16,8,8192]{2,1,0:T(8,128)(2,1)} reshape(bf16[128,64,128]{2,1,0:T(8,128)(2,1)S(1)} %copy.24) | data formatting | bytes 4194304 | tf_op jit(solution)/shard_map/reshape;reshape | solution.py:109
  123.6 34.7 %all_to_all.10 = bf16[16,8,8192]{2,1,0:T(8,128)(2,1)S(1)} all-to-all(bf16[16,8,8192]{2,1,0:T(8,128)(2,1)} %reshape_reshape.7), channel_id=1, replica_groups=mesh['dp'=16,'tensor'=16] {'tensor'}, dimensions={0} | all-to-all | bytes 4194304 | tf_op jit(solution)/shard_map/all_to_all | solution.py:110
  158.3 1.0 reduce_sum.38
  159.3 42.5 %reduce-scatter.2.cloned.1.call-done = bf16[13,2,128,128]{3,2,1,0:T(8,128)(2,1)} async-done(((bf16[208,2,128,128]{3,2,1,0:T(8,128)(2,1)}), bf16[13,2,128,128]{3,2,1,0:T(8,128)(2,1)}) %reduce-scatter.2.cloned.1.call-update) | async-done | bytes 851984 | tf_op jit(solution)/shard_map/reduce_scatter | solution.py:112
  201.7 2.1 %slice_bitcast_fusion = (bf16[1,13,128,128]{3,2,1,0:T(8,128)(2,1)}, bf16[1,13,128,128]{3,2,1,0:T(8,128)(2,1)}) fusion(bf16[13,2,128,128]{3,2,1,0:T(8,128)(2,1)} %reduce-scatter.2.cloned.1.call-done), kind=kLoop, calls=%fused_computation.2 | loop fusion | bytes 1703936 | tf_op jit(solution)/shard_map/broadcast_in_dim;squeeze | solution.py:114
  (14 shorter events, 0.2 us)
Async XLA Ops:
  7.2 2.3 %copy-start.1 = (bf16[8,8192]{1,0:T(8,128)(2,1)S(1)}, bf16[8,8192]{1,0:T(8,128)(2,1)}, u32[]{:S(2)}) copy-start(bf16[8,8192]{1,0:T(8,128)(2,1)} %param.6) | copy-start | bytes 393220
  7.2 86.1 %all-gather.2.cloned.1.call-start = ((), (), s32[]{:S(2)}) async-start(), calls=%async_computation.3 | async-start | bytes 14483456 | tf_op jit(solution)/shard_map/all_gather | solution.py:104
  10.9 7.7 %copy-start.2 = (s32[2,7,16]{2,0,1:T(2,128)S(1)}, s32[2,7,16]{2,0,1:T(2,128)}, u32[]{:S(2)}) copy-start(s32[2,7,16]{2,0,1:T(2,128)} %param.10) | copy-start | bytes 2692
  10.9 8.3 %copy-start.3 = (s32[2,7,16]{2,0,1:T(2,128)S(1)}, s32[2,7,16]{2,0,1:T(2,128)}, u32[]{:S(2)}) copy-start(s32[2,7,16]{2,0,1:T(2,128)} %param.11) | copy-start | bytes 2692
  10.9 34.7 %all-to-all-start = ((bf16[16,8,8192]{2,1,0:T(8,128)(2,1)}), bf16[16,8,8192]{2,1,0:T(8,128)(2,1)S(1)}, u32[]{:S(2)}, u32[]{:S(2)}) async-start(bf16[16,8,8192]{2,1,0:T(8,128)(2,1)} %broadcast_in_dim.2), calls=%async_computation | async-start | bytes 4194304 | tf_op jit(solution)/shard_map/all_to_all | solution.py:86
  18.5 183.2 %reduce-scatter.2.cloned.1.call-start = ((), (), s32[]{:S(2)}) async-start(), calls=%async_computation.4 | async-start | bytes 14483456 | tf_op jit(solution)/shard_map/reduce_scatter | solution.py:112
  45.7 1.3 copy-start
Sparse Core Ops, SparseCore 0:
  9.8 83.4 all-gather.1
  118.4 83.2 reduce-scatter.1

commit v3 on v2

--- a/solution.py
+++ b/solution.py
@@ -16,20 +16,43 @@
     return owner_ids * capacity + tile_ranks
 
 
-def _swiglu_kernel(rows_ref, slots_ref, tok_ref, tokt_ref, store_ref, hgrad_ref,
-                   hidden_ref, tpart_ref, grad_ref, acc_ref, delta_ref):
+def _swiglu_kernel(rows_ref, slots_ref, tok_ref, tokt_ref, store_hbm, hgrad_ref, zero_hbm,
+                   hidden_ref, tpart_ref, grad_hbm, acc_ref, delta_ref, panel_ref, term_ref,
+                   in_sem, out_sem):
+    del zero_hbm
     group_blocks = hgrad_ref.shape[1] // 128
-    per_block = rows_ref.shape[1] // group_blocks
+    tile_count = rows_ref.shape[1]
+    per_block = tile_count // group_blocks
+
+    def tile_copy_in(m, i):
+        s = slots_ref[m, i]
+        return pltpu.make_async_copy(store_hbm.at[s, m], panel_ref.at[m, i],
+                                     in_sem.at[m * tile_count + i])
+
+    def tile_copy_out(m, i):
+        s = slots_ref[m, i]
+        return pltpu.make_async_copy(term_ref.at[m, i], grad_hbm.at[s, m],
+                                     out_sem.at[m * tile_count + i])
+
+    def start_in(i, carry):
+        for m in range(2):
+            tile_copy_in(m, i).start()
+        return carry
+    lax.fori_loop(0, tile_count, start_in, 0)
     acc_ref[...] = jnp.zeros(acc_ref.shape, jnp.float32)
-    grad_ref[...] = jnp.zeros(grad_ref.shape, grad_ref.dtype)
     for f in range(group_blocks):
+        def wait_in(k, carry, f=f):
+            for m in range(2):
+                tile_copy_in(m, f * per_block + k).wait()
+            return carry
+        lax.fori_loop(0, per_block, wait_in, 0)
         pre = []
         for m in range(2):
-            def fwd_step(k, carry, m=m):
+            def fwd_step(k, carry, m=m, f=f):
                 i = f * per_block + k
                 r = rows_ref[m, i]
-                s = slots_ref[m, i]
-                return carry + jnp.dot(tok_ref[r], store_ref[s, m], preferred_element_type=jnp.float32)
+                return carry + jnp.dot(tok_ref[r], panel_ref[m, i],
+                                       preferred_element_type=jnp.float32)
             pre.append(lax.fori_loop(0, per_block, fwd_step,
                                      jnp.zeros((128, 128), jnp.float32), unroll=True))
         gate_pre, up_pre = pre
@@ -40,42 +63,55 @@
         delta_ref[0] = (hg * up_pre * sig * (1.0 + gate_pre * (1.0 - sig))).astype(delta_ref.dtype)
         delta_ref[1] = (hg * gate_pre * sig).astype(delta_ref.dtype)
 
-        def back_step(k, carry):
+        def back_step(k, carry, f=f):
             i = f * per_block + k
             for m in range(2):
                 r = rows_ref[m, i]
-                s = slots_ref[m, i]
                 d = delta_ref[m]
-                back = lax.dot_general(d, store_ref[s, m], (((1,), (1,)), ((), ())),
+                back = lax.dot_general(d, panel_ref[m, i], (((1,), (1,)), ((), ())),
                                        preferred_element_type=jnp.float32)
                 acc_ref[r] = acc_ref[r] + back
                 term = jnp.dot(tokt_ref[r], d, preferred_element_type=jnp.float32)
-                grad_ref[s, m] = term.astype(grad_ref.dtype)
+                term_ref[m, i] = term.astype(term_ref.dtype)
+                tile_copy_out(m, i).start()
             return carry
         lax.fori_loop(0, per_block, back_step, 0, unroll=True)
     tpart_ref[...] = acc_ref[...].astype(tpart_ref.dtype)
 
+    def wait_out(i, carry):
+        for m in range(2):
+            tile_copy_out(m, i).wait()
+        return carry
+    lax.fori_loop(0, tile_count, wait_out, 0)
+
 
 def swiglu_local(rows, slots, tok_bm, tokt_bm, store, hgrad, interpret=False):
     row_blocks, tok_count, tile = tok_bm.shape
-    slot_total = store.shape[0]
+    tile_count = rows.shape[1]
     smem = pl.BlockSpec(memory_space=pltpu.SMEM)
     vmem = pl.BlockSpec(memory_space=pltpu.VMEM)
+    hbm = pl.BlockSpec(memory_space=pl.ANY)
+    zero_grads = jnp.zeros(store.shape, jnp.bfloat16)
     out_shape = (
         jax.ShapeDtypeStruct(hgrad.shape, jnp.bfloat16),
         jax.ShapeDtypeStruct((row_blocks, tok_count, tile), jnp.bfloat16),
-        jax.ShapeDtypeStruct((slot_total, 2, tile, tile), jnp.bfloat16),
+        jax.ShapeDtypeStruct(store.shape, jnp.bfloat16),
     )
     return pl.pallas_call(
         _swiglu_kernel,
         out_shape=out_shape,
-        in_specs=[smem, smem, vmem, vmem, vmem, vmem],
-        out_specs=(vmem, vmem, vmem),
+        in_specs=[smem, smem, vmem, vmem, hbm, vmem, hbm],
+        out_specs=(vmem, vmem, hbm),
         scratch_shapes=[pltpu.VMEM((row_blocks, tok_count, tile), jnp.float32),
-                        pltpu.VMEM((2, tok_count, tile), jnp.bfloat16)],
+                        pltpu.VMEM((2, tok_count, tile), jnp.bfloat16),
+                        pltpu.VMEM((2, tile_count, tile, tile), jnp.bfloat16),
+                        pltpu.VMEM((2, tile_count, tile, tile), jnp.bfloat16),
+                        pltpu.SemaphoreType.DMA((2 * tile_count,)),
+                        pltpu.SemaphoreType.DMA((2 * tile_count,))],
+        input_output_aliases={6: 2},
         compiler_params=pltpu.CompilerParams(vmem_limit_bytes=100 * 1024 * 1024),
         interpret=interpret,
-    )(rows, slots, tok_bm, tokt_bm, store, hgrad)
+    )(rows, slots, tok_bm, tokt_bm, store, hgrad, zero_grads)
 
 
 def body(tokens, hidden_grad, gate_tiles, up_tiles, tile_rows, tile_owner):

time: 211 us -> 218 us (1.033)
  local copies, waits for them, and re-layouts: 19 us -> 27.4 us
    broadcast_in_dim x0 -> x1, local copies, waits for them, and re-layouts: none -> 8.4 us  [swiglu_local(): zero_grads = jnp.zeros(store.shape, jnp.bfloat16)]
where the time goes in v3:
time: 218 us; the launch traced here: 217 us
  waiting for transfers between devices  106 us (49%)
  blocking collectives  34.7 us (16%)
  local copies, waits for them, and re-layouts  27.4 us (13%)
  Pallas kernels  23.4 us (11%)
  between operations  14.1 us (6%)
  starting transfers between devices  7.68 us (4%)
  other arithmetic  4.12 us (2%)
    reduce_scatter x1, waiting for transfers between devices, body(): tile_sums = lax.psum_scatter(grads, 'dp', scatter_dimension=0, tiled=True)  42.5 us
    all_gather x1, waiting for transfers between devices, body(): store = lax.all_gather(local_pair, 'dp', axis=0, tiled=True)  38.5 us
    all_to_all x1, blocking collectives, body(): part_recv = lax.all_to_all(part_rows, 'tensor', 0, 0, tiled=True)  34.7 us
    all_to_all x1, waiting for transfers between devices, body(): lax.all_to_all(tok_copies, 'tensor', 0, 0, tiled=True)  25.1 us
    pallas_call x1, Pallas kernels, swiglu_local(): pl.pallas_call(_swiglu_kernel, out_shape=out_shape, in_specs=[smem, smem,...  23.4 us
    broadcast_in_dim x1, local copies, waits for them, and re-layouts, swiglu_local(): zero_grads = jnp.zeros(store.shape, jnp.bfloat16)  8.4 us
    all_to_all x1, starting transfers between devices, body(): lax.all_to_all(tok_copies, 'tensor', 0, 0, tiled=True)  7.61 us
    another operation x2, local copies, waits for them, and re-layouts, body(): tok_blocks = gathered_tok.reshape(tok_count, row_blocks, tile_size)  5.61 us
  transfers between devices with their start and end apart: 3, of which 3 were waited for; matrix products, arithmetic and copies ran while one was open for 8% of the time, Pallas kernels for 0%

profile of v3, /device:TPU:2, one launch (start us, length us, event | category | flops | bytes accessed | tf_op | source)
XLA Modules:
  0.0 217.5 jit_solution(1921058045680206902)
XLA Ops:
  7.2 2.2 %pad_maximum_fusion = bf16[13,2,128,128]{3,2,1,0:T(8,128)(2,1)} fusion(bf16[13,1,128,128]{3,2,1,0:T(8,128)(2,1)} %bitcast.24, bf16[13,1,128,128]{3,2,1,0:T(8,128)(2,1)} %bitcast.25), kind=kLoop, calls=%fused_computation.1 | loop fusion | flops 425984 | bytes 1703936 | tf_op jit(solution)/shard_map/stack | solution.py:139
  9.4 1.5 broadcast_in_dim.4
  10.9 7.6 %all-to-all-start = ((bf16[16,8,8192]{2,1,0:T(8,128)(2,1)}), bf16[16,8,8192]{2,1,0:T(8,128)(2,1)S(1)}, u32[]{:S(2)}, u32[]{:S(2)}) async-start(bf16[16,8,8192]{2,1,0:T(8,128)(2,1)} %broadcast_in_dim.4), calls=%async_computation | async-start | bytes 4194304 | tf_op jit(solution)/shard_map/all_to_all | solution.py:122
  18.6 0.6 reshape.54.rows_ref
  19.3 0.1 eq.30
  19.4 0.1 eq.34
  19.5 0.1 mul.29
  19.6 0.2 convert_reduce_fusion.1
  19.8 0.2 convert_reduce_fusion
  20.0 0.6 pad_add_fusion.slots_ref
  20.6 25.1 %all-to-all-done = bf16[16,8,8192]{2,1,0:T(8,128)(2,1)S(1)} async-done(((bf16[16,8,8192]{2,1,0:T(8,128)(2,1)}), bf16[16,8,8192]{2,1,0:T(8,128)(2,1)S(1)}, u32[]{:S(2)}, u32[]{:S(2)}) %all-to-all-start) | async-done | bytes 2097184 | tf_op jit(solution)/shard_map/all_to_all | solution.py:122
  45.7 1.3 copy-done
  47.0 2.2 %copy.26 = bf16[16,8,64,128]{3,2,1,0:T(8,128)(2,1)S(1)} copy(bf16[16,8,64,128]{3,1,2,0:T(8,128)(2,1)} %bitcast.22) | data formatting | bytes 4194304
  49.2 3.0 %copy.24 = bf16[128,64,128]{0,2,1:T(8,128)(2,1)} copy(bf16[128,64,128]{2,1,0:T(8,128)(2,1)S(1)} %bitcast.18) | data formatting | bytes 4194304 | tf_op jit(solution)/shard_map/reshape;reshape | solution.py:127
  52.2 2.6 %copy.28 = bf16[128,64,128]{2,0,1:T(8,128)(2,1)} copy(bf16[128,64,128]{2,1,0:T(8,128)(2,1)S(1)} %bitcast.19) | data formatting | bytes 4194304 | tf_op jit(solution)/shard_map/reshape;reshape | solution.py:127
  54.8 38.5 %all-gather.2.cloned.1.call-done.store_hbm = bf16[208,2,128,128]{3,2,1,0:T(8,128)(2,1)} async-done(((bf16[13,2,128,128]{3,2,1,0:T(8,128)(2,1)}), bf16[208,2,128,128]{3,2,1,0:T(8,128)(2,1)}) %all-gather.2.cloned.1.call-update) | async-done | bytes 13631504 | tf_op jit(solution)/shard_map/all_gather | solution.py:140
  93.3 8.4 %broadcast_in_dim.5.zero_hbm = bf16[208,2,128,128]{3,2,1,0:T(8,128)(2,1)} broadcast(bf16[]{:T(256)} %constant.2.clone.1), dimensions={} | broadcast | bytes 13631490 | tf_op jit(solution)/shard_map/broadcast_in_dim | solution.py:94
  101.7 23.4 %shard_map.93 = (bf16[128,896]{1,0:T(8,128)(2,1)}, bf16[64,128,128]{2,1,0:T(8,128)(2,1)}, bf16[208,2,128,128]{3,2,1,0:T(8,128)(2,1)}) custom-call(s32[2,112]{1,0:T(2,128)} %reshape.54.rows_ref, s32[2,112]{1,0:T(2,128)} %pad_add_fusion.slots_ref, bf16[64,128,128]{2,1,0:T(8,128)(2,1)} %bitcast.21, ...), custom_call_target="tpu_custom_call", output_to_operand_aliasing={{2}: (6, {})} | custom-call | tf_op jit(solution)/shard_map/pallas_call | solution.py:100
  125.1 2.9 %copy.25 = bf16[128,64,128]{2,1,0:T(8,128)(2,1)S(1)} copy(bf16[128,64,128]{2,0,1:T(8,128)(2,1)} %bitcast.23) | data formatting | bytes 4194304 | tf_op jit(solution)/shard_map/transpose | solution.py:144
  128.1 2.3 %reshape_reshape.7 = bf16[16,8,8192]{2,1,0:T(8,128)(2,1)} reshape(bf16[128,64,128]{2,1,0:T(8,128)(2,1)S(1)} %copy.25) | data formatting | bytes 4194304 | tf_op jit(solution)/shard_map/reshape;reshape | solution.py:145
  130.4 34.7 %all_to_all.10 = bf16[16,8,8192]{2,1,0:T(8,128)(2,1)S(1)} all-to-all(bf16[16,8,8192]{2,1,0:T(8,128)(2,1)} %reshape_reshape.7), channel_id=1, replica_groups=mesh['dp'=16,'tensor'=16] {'tensor'}, dimensions={0} | all-to-all | bytes 4194304 | tf_op jit(solution)/shard_map/all_to_all | solution.py:146
  165.1 1.0 reduce_sum.38
  166.1 42.5 %reduce-scatter.2.cloned.1.call-done = bf16[13,2,128,128]{3,2,1,0:T(8,128)(2,1)} async-done(((bf16[208,2,128,128]{3,2,1,0:T(8,128)(2,1)}), bf16[13,2,128,128]{3,2,1,0:T(8,128)(2,1)}) %reduce-scatter.2.cloned.1.call-update) | async-done | bytes 851984 | tf_op jit(solution)/shard_map/reduce_scatter | solution.py:148
  208.5 2.1 slice_bitcast_fusion
  (15 shorter events, 0.3 us)
Async XLA Ops:
  7.2 2.3 %copy-start.1 = (bf16[8,8192]{1,0:T(8,128)(2,1)S(1)}, bf16[8,8192]{1,0:T(8,128)(2,1)}, u32[]{:S(2)}) copy-start(bf16[8,8192]{1,0:T(8,128)(2,1)} %param.6) | copy-start | bytes 393220
  7.2 86.1 %all-gather.2.cloned.1.call-start = ((), (), s32[]{:S(2)}) async-start(), calls=%async_computation.3 | async-start | bytes 14483456 | tf_op jit(solution)/shard_map/all_gather | solution.py:140
  10.9 7.7 %copy-start.2 = (s32[2,7,16]{2,0,1:T(2,128)S(1)}, s32[2,7,16]{2,0,1:T(2,128)}, u32[]{:S(2)}) copy-start(s32[2,7,16]{2,0,1:T(2,128)} %param.10) | copy-start | bytes 2692
  10.9 8.3 %copy-start.3 = (s32[2,7,16]{2,0,1:T(2,128)S(1)}, s32[2,7,16]{2,0,1:T(2,128)}, u32[]{:S(2)}) copy-start(s32[2,7,16]{2,0,1:T(2,128)} %param.11) | copy-start | bytes 2692
  10.9 34.7 %all-to-all-start = ((bf16[16,8,8192]{2,1,0:T(8,128)(2,1)}), bf16[16,8,8192]{2,1,0:T(8,128)(2,1)S(1)}, u32[]{:S(2)}, u32[]{:S(2)}) async-start(bf16[16,8,8192]{2,1,0:T(8,128)(2,1)} %broadcast_in_dim.4), calls=%async_computation | async-start | bytes 4194304 | tf_op jit(solution)/shard_map/all_to_all | solution.py:122
  18.5 190.0 %reduce-scatter.2.cloned.1.call-start = ((), (), s32[]{:S(2)}) async-start(), calls=%async_computation.4 | async-start | bytes 14483456 | tf_op jit(solution)/shard_map/reduce_scatter | solution.py:148
  45.7 1.3 copy-start
Sparse Core Ops, SparseCore 0:
  9.8 83.4 all-gather.1
  125.2 83.2 reduce-scatter.1

commit v4 on v3

--- a/solution.py
+++ b/solution.py
@@ -16,13 +16,14 @@
     return owner_ids * capacity + tile_ranks
 
 
-def _swiglu_kernel(rows_ref, slots_ref, tok_ref, tokt_ref, store_hbm, hgrad_ref, zero_hbm,
-                   hidden_ref, tpart_ref, grad_hbm, acc_ref, delta_ref, panel_ref, term_ref,
-                   in_sem, out_sem):
-    del zero_hbm
+def _swiglu_kernel(rows_ref, slots_ref, free_ref, tok_ref, tokt_ref, store_hbm, hgrad_ref,
+                   hidden_ref, tpart_ref, grad_hbm, acc_ref, panel_ref, term_ref, picked_ref,
+                   zero_ref, in_sem, out_sem, zero_sem):
     group_blocks = hgrad_ref.shape[1] // 128
     tile_count = rows_ref.shape[1]
+    free_count = free_ref.shape[1]
     per_block = tile_count // group_blocks
+    tile = panel_ref.shape[2]
 
     def tile_copy_in(m, i):
         s = slots_ref[m, i]
@@ -34,11 +35,22 @@
         return pltpu.make_async_copy(term_ref.at[m, i], grad_hbm.at[s, m],
                                      out_sem.at[m * tile_count + i])
 
+    def zero_copy(m, j):
+        u = free_ref[m, j]
+        return pltpu.make_async_copy(zero_ref, grad_hbm.at[u, m], zero_sem.at[m * free_count + j])
+
     def start_in(i, carry):
         for m in range(2):
             tile_copy_in(m, i).start()
         return carry
     lax.fori_loop(0, tile_count, start_in, 0)
+    zero_ref[...] = jnp.zeros(zero_ref.shape, zero_ref.dtype)
+
+    def start_zero(j, carry):
+        for m in range(2):
+            zero_copy(m, j).start()
+        return carry
+    lax.fori_loop(0, free_count, start_zero, 0)
     acc_ref[...] = jnp.zeros(acc_ref.shape, jnp.float32)
     for f in range(group_blocks):
         def wait_in(k, carry, f=f):
@@ -54,28 +66,28 @@
                 return carry + jnp.dot(tok_ref[r], panel_ref[m, i],
                                        preferred_element_type=jnp.float32)
             pre.append(lax.fori_loop(0, per_block, fwd_step,
-                                     jnp.zeros((128, 128), jnp.float32), unroll=True))
+                                     jnp.zeros((tile, tile), jnp.float32), unroll=True))
         gate_pre, up_pre = pre
-        cols = slice(f * 128, (f + 1) * 128)
+        cols = slice(f * tile, (f + 1) * tile)
         hg = hgrad_ref[:, cols].astype(jnp.float32)
         sig = 1.0 / (1.0 + jnp.exp(-gate_pre))
         hidden_ref[:, cols] = (gate_pre * sig * up_pre).astype(hidden_ref.dtype)
-        delta_ref[0] = (hg * up_pre * sig * (1.0 + gate_pre * (1.0 - sig))).astype(delta_ref.dtype)
-        delta_ref[1] = (hg * gate_pre * sig).astype(delta_ref.dtype)
-
-        def back_step(k, carry, f=f):
-            i = f * per_block + k
-            for m in range(2):
+        gate_delta = (hg * up_pre * sig * (1.0 + gate_pre * (1.0 - sig))).astype(jnp.bfloat16)
+        up_delta = (hg * gate_pre * sig).astype(jnp.bfloat16)
+        for m, delta in ((0, gate_delta), (1, up_delta)):
+            delta_t = delta.astype(jnp.float32).T.astype(jnp.bfloat16)
+            for k in range(per_block):
+                r = rows_ref[m, f * per_block + k]
+                picked_ref[k * tile:(k + 1) * tile, :] = tokt_ref[r]
+            panel = panel_ref[m, f * per_block:(f + 1) * per_block].reshape(per_block * tile, tile)
+            back_t = jnp.dot(panel, delta_t, preferred_element_type=jnp.float32)
+            term = jnp.dot(picked_ref[...], delta, preferred_element_type=jnp.float32)
+            for k in range(per_block):
+                i = f * per_block + k
                 r = rows_ref[m, i]
-                d = delta_ref[m]
-                back = lax.dot_general(d, panel_ref[m, i], (((1,), (1,)), ((), ())),
-                                       preferred_element_type=jnp.float32)
-                acc_ref[r] = acc_ref[r] + back
-                term = jnp.dot(tokt_ref[r], d, preferred_element_type=jnp.float32)
-                term_ref[m, i] = term.astype(term_ref.dtype)
+                acc_ref[r] = acc_ref[r] + back_t[k * tile:(k + 1) * tile]
+                term_ref[m, i] = term[k * tile:(k + 1) * tile].astype(term_ref.dtype)
                 tile_copy_out(m, i).start()
-            return carry
-        lax.fori_loop(0, per_block, back_step, 0, unroll=True)
     tpart_ref[...] = acc_ref[...].astype(tpart_ref.dtype)
 
     def wait_out(i, carry):
@@ -84,34 +96,48 @@
         return carry
     lax.fori_loop(0, tile_count, wait_out, 0)
 
-
-def swiglu_local(rows, slots, tok_bm, tokt_bm, store, hgrad, interpret=False):
+    def wait_zero(j, carry):
+        for m in range(2):
+            zero_copy(m, j).wait()
+        return carry
+    lax.fori_loop(0, free_count, wait_zero, 0)
+
+
+def swiglu_local(rows, slots, free, tok_bm, tokt_bm, store, hgrad, interpret=False):
     row_blocks, tok_count, tile = tok_bm.shape
     tile_count = rows.shape[1]
+    free_count = free.shape[1]
     smem = pl.BlockSpec(memory_space=pltpu.SMEM)
     vmem = pl.BlockSpec(memory_space=pltpu.VMEM)
     hbm = pl.BlockSpec(memory_space=pl.ANY)
-    zero_grads = jnp.zeros(store.shape, jnp.bfloat16)
     out_shape = (
         jax.ShapeDtypeStruct(hgrad.shape, jnp.bfloat16),
-        jax.ShapeDtypeStruct((row_blocks, tok_count, tile), jnp.bfloat16),
+        jax.ShapeDtypeStruct((row_blocks, tile, tok_count), jnp.bfloat16),
         jax.ShapeDtypeStruct(store.shape, jnp.bfloat16),
     )
     return pl.pallas_call(
         _swiglu_kernel,
         out_shape=out_shape,
-        in_specs=[smem, smem, vmem, vmem, hbm, vmem, hbm],
+        in_specs=[smem, smem, smem, vmem, vmem, hbm, vmem],
         out_specs=(vmem, vmem, hbm),
-        scratch_shapes=[pltpu.VMEM((row_blocks, tok_count, tile), jnp.float32),
-                        pltpu.VMEM((2, tok_count, tile), jnp.bfloat16),
+        scratch_shapes=[pltpu.VMEM((row_blocks, tile, tok_count), jnp.float32),
                         pltpu.VMEM((2, tile_count, tile, tile), jnp.bfloat16),
                         pltpu.VMEM((2, tile_count, tile, tile), jnp.bfloat16),
+                        pltpu.VMEM((tile_count // (hgrad.shape[1] // tile) * tile, tok_count), jnp.bfloat16),
+                        pltpu.VMEM((tile, tile), jnp.bfloat16),
                         pltpu.SemaphoreType.DMA((2 * tile_count,)),
-                        pltpu.SemaphoreType.DMA((2 * tile_count,))],
-        input_output_aliases={6: 2},
+                        pltpu.SemaphoreType.DMA((2 * tile_count,)),
+                        pltpu.SemaphoreType.DMA((2 * free_count,))],
         compiler_params=pltpu.CompilerParams(vmem_limit_bytes=100 * 1024 * 1024),
         interpret=interpret,
-    )(rows, slots, tok_bm, tokt_bm, store, hgrad, zero_grads)
+    )(rows, slots, free, tok_bm, tokt_bm, store, hgrad)
+
+
+def free_slots(slots, slot_total):
+    taken = jnp.zeros((slots.shape[0], slot_total), jnp.int32).at[
+        jnp.arange(slots.shape[0])[:, None], slots].set(1)
+    order = jnp.argsort(taken, axis=1, stable=True).astype(jnp.int32)
+    return order[:, : slot_total - slots.shape[1]]
 
 
 def body(tokens, hidden_grad, gate_tiles, up_tiles, tile_rows, tile_owner):
@@ -138,10 +164,11 @@
     )
     local_pair = jnp.stack([gate_tiles[0], up_tiles[0]], axis=1)
     store = lax.all_gather(local_pair, "dp", axis=0, tiled=True)
-    hidden, tpart_bm, grads = swiglu_local(
-        row_flat, slot_stack, tok_bm, tokt_bm, store, hidden_grad
-    )
-    token_part = tpart_bm.transpose(1, 0, 2).reshape(tok_count, model_width)
+    free = free_slots(slot_stack, store.shape[0])
+    hidden, tpart_t, grads = swiglu_local(
+        row_flat, slot_stack, free, tok_bm, tokt_bm, store, hidden_grad
+    )
+    token_part = tpart_t.transpose(2, 0, 1).reshape(tok_count, model_width)
     part_rows = token_part.reshape(tensor_count, tok_count // tensor_count, model_width)
     part_recv = lax.all_to_all(part_rows, "tensor", 0, 0, tiled=True)
     token_grad = jnp.sum(part_recv.astype(jnp.float32), axis=0).astype(jnp.bfloat16)

time: 218 us -> 209 us (0.959)
  waiting for transfers between devices: 106 us -> 90.1 us
  local copies, waits for them, and re-layouts: 27.4 us -> 31.7 us
  other arithmetic: 4.12 us -> 7.41 us
    all_to_all x1, waiting for transfers between devices: 25.1 us -> 9.43 us  [body(): lax.all_to_all(tok_copies, 'tensor', 0, 0, tiled=True)]
    scatter x0 -> x1, local copies, waits for them, and re-layouts: none -> 11.7 us  [free_slots(): taken = jnp.zeros((slots.shape[0], slot_total), jnp.int32).at[jnp.arange(...]
    broadcast_in_dim x1 -> x2, local copies, waits for them, and re-layouts: 8.4 us -> 0.01 us  [the longest x1 0.01 us: free_slots(): taken = jnp.zeros((slots.shape[0], slot_total), jnp.int32).at[jnp.arange(...]
    sort x0 -> x1, other arithmetic: none -> 3.27 us  [free_slots(): order = jnp.argsort(taken, axis=1, stable=True).astype(jnp.int32)]
  transfers between devices with their start and end apart: 3 -> 3, of which waited for: 3 -> 3; matrix products, arithmetic and copies ran while one was open for 8% -> 16% of each run, Pallas kernels for 0% -> 0%
where the time goes in v4:
time: 209 us
  waiting for transfers between devices  90.1 us (43%)
  blocking collectives  34.7 us (17%)
  local copies, waits for them, and re-layouts  31.7 us (15%)
  Pallas kernels  23.1 us (11%)
  between operations  14.1 us (7%)
  starting transfers between devices  7.68 us (4%)
  other arithmetic  7.41 us (4%)
    reduce_scatter x1, waiting for transfers between devices, body(): tile_sums = lax.psum_scatter(grads, 'dp', scatter_dimension=0, tiled=True)  42.1 us
    all_gather x1, waiting for transfers between devices, body(): store = lax.all_gather(local_pair, 'dp', axis=0, tiled=True)  38.5 us
    all_to_all x1, blocking collectives, body(): part_recv = lax.all_to_all(part_rows, 'tensor', 0, 0, tiled=True)  34.7 us
    pallas_call x1, Pallas kernels, swiglu_local(): pl.pallas_call(_swiglu_kernel, out_shape=out_shape, in_specs=[smem, smem,...  23.1 us
    scatter x1, local copies, waits for them, and re-layouts, free_slots(): taken = jnp.zeros((slots.shape[0], slot_total), jnp.int32).at[jnp.arange(...  11.7 us
    all_to_all x1, waiting for transfers between devices, body(): lax.all_to_all(tok_copies, 'tensor', 0, 0, tiled=True)  9.43 us
    all_to_all x1, starting transfers between devices, body(): lax.all_to_all(tok_copies, 'tensor', 0, 0, tiled=True)  7.61 us
    another operation x2, local copies, waits for them, and re-layouts, body(): tok_blocks = gathered_tok.reshape(tok_count, row_blocks, tile_size)  5.61 us
  transfers between devices with their start and end apart: 3, of which 3 were waited for; matrix products, arithmetic and copies ran while one was open for 16% of the time, Pallas kernels for 0%

profile of v4, /device:TPU:2, one launch (start us, length us, event | category | flops | bytes accessed | tf_op | source)
XLA Modules:
  0.0 208.8 jit_solution(15972147444229477475)
XLA Ops:
  7.2 2.2 %pad_maximum_fusion = bf16[13,2,128,128]{3,2,1,0:T(8,128)(2,1)} fusion(bf16[13,1,128,128]{3,2,1,0:T(8,128)(2,1)} %bitcast.27, bf16[13,1,128,128]{3,2,1,0:T(8,128)(2,1)} %bitcast.28), kind=kLoop, calls=%fused_computation.2 | loop fusion | flops 425984 | bytes 1703936 | tf_op jit(solution)/shard_map/stack | solution.py:165
  9.4 1.5 broadcast_in_dim.11
  10.9 7.6 %all-to-all-start = ((bf16[16,8,8192]{2,1,0:T(8,128)(2,1)}), bf16[16,8,8192]{2,1,0:T(8,128)(2,1)S(1)}, u32[]{:S(2)}, u32[]{:S(2)}) async-start(bf16[16,8,8192]{2,1,0:T(8,128)(2,1)} %broadcast_in_dim.11), calls=%async_computation | async-start | bytes 4194304 | tf_op jit(solution)/shard_map/all_to_all | solution.py:148
  18.6 0.6 reshape.151.rows_ref
  19.6 0.2 convert_reduce_fusion.1
  19.8 0.2 convert_reduce_fusion
  20.0 0.1 reshape.152
  20.1 11.7 %scatter_fusion = s32[2,208]{1,0:T(2,128)S(1)} fusion(s32[2,208]{1,0:T(2,128)S(1)} %broadcast_in_dim.8, s32[224]{0:T(256)S(1)} %reshape.152, s32[224]{0:T(256)S(1)} %broadcast.81), kind=kCustom, calls=%fused_computation | custom fusion | bytes 4480 | tf_op jit(solution)/shard_map/scatter | solution.py:138
  31.8 3.3 %sort.17 = (s32[2,208]{1,0:T(2,128)}, s32[2,208]{1,0:T(2,128)S(1)}) sort(s32[2,208]{1,0:T(2,128)S(1)} %scatter_fusion, s32[2,208]{1,0:T(2,128)S(1)} %iota.18), dimensions={1}, to_apply=%region_3.0 | sort | flops 3744 | bytes 6656 | tf_op jit(solution)/shard_map/jit(argsort)/sort | solution.py:139
  35.1 0.6 slice.17.free_ref
  35.7 0.6 pad_add_fusion.slots_ref
  36.2 9.4 %all-to-all-done = bf16[16,8,8192]{2,1,0:T(8,128)(2,1)S(1)} async-done(((bf16[16,8,8192]{2,1,0:T(8,128)(2,1)}), bf16[16,8,8192]{2,1,0:T(8,128)(2,1)S(1)}, u32[]{:S(2)}, u32[]{:S(2)}) %all-to-all-start) | async-done | bytes 2097184 | tf_op jit(solution)/shard_map/all_to_all | solution.py:148
  45.7 1.3 copy-done
  47.0 2.2 %copy.25 = bf16[16,8,64,128]{3,2,1,0:T(8,128)(2,1)S(1)} copy(bf16[16,8,64,128]{3,1,2,0:T(8,128)(2,1)} %bitcast.25) | data formatting | bytes 4194304
  49.2 3.0 %copy.23 = bf16[128,64,128]{0,2,1:T(8,128)(2,1)} copy(bf16[128,64,128]{2,1,0:T(8,128)(2,1)S(1)} %bitcast.21) | data formatting | bytes 4194304 | tf_op jit(solution)/shard_map/reshape;reshape | solution.py:153
  52.2 2.6 %copy.27 = bf16[128,64,128]{2,0,1:T(8,128)(2,1)} copy(bf16[128,64,128]{2,1,0:T(8,128)(2,1)S(1)} %bitcast.22) | data formatting | bytes 4194304 | tf_op jit(solution)/shard_map/reshape;reshape | solution.py:153
  54.8 38.5 %all-gather.2.cloned.1.call-done.store_hbm = bf16[208,2,128,128]{3,2,1,0:T(8,128)(2,1)} async-done(((bf16[13,2,128,128]{3,2,1,0:T(8,128)(2,1)}), bf16[208,2,128,128]{3,2,1,0:T(8,128)(2,1)}) %all-gather.2.cloned.1.call-update) | async-done | bytes 13631504 | tf_op jit(solution)/shard_map/all_gather | solution.py:166
  93.3 23.1 %shard_map.93 = (bf16[128,896]{1,0:T(8,128)(2,1)}, bf16[64,128,128]{2,1,0:T(8,128)(2,1)}, bf16[208,2,128,128]{3,2,1,0:T(8,128)(2,1)}) custom-call(s32[2,112]{1,0:T(2,128)} %reshape.151.rows_ref, s32[2,112]{1,0:T(2,128)} %pad_add_fusion.slots_ref, s32[2,96]{1,0:T(2,128)} %slice.17.free_ref, bf16[64,128,128]{2,1,0:T(8,128)(2,1)} %bitcast.24, ...), custom_call_target="tpu_custom_call" | custom-call | tf_op jit(solution)/shard_map/pallas_call | solution.py:118
  116.5 3.3 %copy.24 = bf16[128,64,128]{2,1,0:T(8,128)(2,1)S(1)} copy(bf16[128,64,128]{0,2,1:T(8,128)(2,1)} %bitcast.26) | data formatting | bytes 4194304 | tf_op jit(solution)/shard_map/transpose | solution.py:171
  119.8 2.3 %reshape_reshape.7 = bf16[16,8,8192]{2,1,0:T(8,128)(2,1)} reshape(bf16[128,64,128]{2,1,0:T(8,128)(2,1)S(1)} %copy.24) | data formatting | bytes 4194304 | tf_op jit(solution)/shard_map/reshape;reshape | solution.py:172
  122.1 34.7 %all_to_all.10 = bf16[16,8,8192]{2,1,0:T(8,128)(2,1)S(1)} all-to-all(bf16[16,8,8192]{2,1,0:T(8,128)(2,1)} %reshape_reshape.7), channel_id=1, replica_groups=mesh['dp'=16,'tensor'=16] {'tensor'}, dimensions={0} | all-to-all | bytes 4194304 | tf_op jit(solution)/shard_map/all_to_all | solution.py:173
  156.8 1.0 reduce_sum.38
  157.8 42.1 %reduce-scatter.2.cloned.1.call-done = bf16[13,2,128,128]{3,2,1,0:T(8,128)(2,1)} async-done(((bf16[208,2,128,128]{3,2,1,0:T(8,128)(2,1)}), bf16[13,2,128,128]{3,2,1,0:T(8,128)(2,1)}) %reduce-scatter.2.cloned.1.call-update) | async-done | bytes 851984 | tf_op jit(solution)/shard_map/reduce_scatter | solution.py:175
  199.9 2.1 %slice_bitcast_fusion = (bf16[1,13,128,128]{3,2,1,0:T(8,128)(2,1)}, bf16[1,13,128,128]{3,2,1,0:T(8,128)(2,1)}) fusion(bf16[13,2,128,128]{3,2,1,0:T(8,128)(2,1)} %reduce-scatter.2.cloned.1.call-done), kind=kLoop, calls=%fused_computation.3 | loop fusion | bytes 1703936 | tf_op jit(solution)/shard_map/broadcast_in_dim;squeeze | solution.py:177
  (22 shorter events, 0.5 us)
Async XLA Ops:
  7.2 2.3 %copy-start.1 = (bf16[8,8192]{1,0:T(8,128)(2,1)S(1)}, bf16[8,8192]{1,0:T(8,128)(2,1)}, u32[]{:S(2)}) copy-start(bf16[8,8192]{1,0:T(8,128)(2,1)} %param.6) | copy-start | bytes 393220
  7.2 86.2 %all-gather.2.cloned.1.call-start = ((), (), s32[]{:S(2)}) async-start(), calls=%async_computation.3 | async-start | bytes 14483456 | tf_op jit(solution)/shard_map/all_gather | solution.py:166
  10.9 7.7 %copy-start.2 = (s32[2,7,16]{2,0,1:T(2,128)S(1)}, s32[2,7,16]{2,0,1:T(2,128)}, u32[]{:S(2)}) copy-start(s32[2,7,16]{2,0,1:T(2,128)} %param.10) | copy-start | bytes 2692
  10.9 8.3 %copy-start.3 = (s32[2,7,16]{2,0,1:T(2,128)S(1)}, s32[2,7,16]{2,0,1:T(2,128)}, u32[]{:S(2)}) copy-start(s32[2,7,16]{2,0,1:T(2,128)} %param.11) | copy-start | bytes 2692
  10.9 34.7 %all-to-all-start = ((bf16[16,8,8192]{2,1,0:T(8,128)(2,1)}), bf16[16,8,8192]{2,1,0:T(8,128)(2,1)S(1)}, u32[]{:S(2)}, u32[]{:S(2)}) async-start(bf16[16,8,8192]{2,1,0:T(8,128)(2,1)} %broadcast_in_dim.11), calls=%async_computation | async-start | bytes 4194304 | tf_op jit(solution)/shard_map/all_to_all | solution.py:148
  18.5 181.3 %reduce-scatter.2.cloned.1.call-start = ((), (), s32[]{:S(2)}) async-start(), calls=%async_computation.4 | async-start | bytes 14483456 | tf_op jit(solution)/shard_map/reduce_scatter | solution.py:175
  45.7 1.3 copy-start
Sparse Core Ops, SparseCore 0:
  9.8 83.4 all-gather.1
  116.6 83.2 reduce-scatter.1

commit v5 on v4

--- a/solution.py
+++ b/solution.py
@@ -16,7 +16,7 @@
     return owner_ids * capacity + tile_ranks
 
 
-def _swiglu_kernel(rows_ref, slots_ref, free_ref, tok_ref, tokt_ref, store_hbm, hgrad_ref,
+def _swiglu_kernel(rows_ref, slots_ref, free_ref, tok_ref, store_hbm, hgrad_ref,
                    hidden_ref, tpart_ref, grad_hbm, acc_ref, panel_ref, term_ref, picked_ref,
                    zero_ref, in_sem, out_sem, zero_sem):
     group_blocks = hgrad_ref.shape[1] // 128
@@ -53,21 +53,20 @@
     lax.fori_loop(0, free_count, start_zero, 0)
     acc_ref[...] = jnp.zeros(acc_ref.shape, jnp.float32)
     for f in range(group_blocks):
+        for m in range(2):
+            for k in range(per_block):
+                r = rows_ref[m, f * per_block + k]
+                picked_ref[m, :, k * tile:(k + 1) * tile] = tok_ref[r]
+
         def wait_in(k, carry, f=f):
             for m in range(2):
                 tile_copy_in(m, f * per_block + k).wait()
             return carry
         lax.fori_loop(0, per_block, wait_in, 0)
-        pre = []
-        for m in range(2):
-            def fwd_step(k, carry, m=m, f=f):
-                i = f * per_block + k
-                r = rows_ref[m, i]
-                return carry + jnp.dot(tok_ref[r], panel_ref[m, i],
-                                       preferred_element_type=jnp.float32)
-            pre.append(lax.fori_loop(0, per_block, fwd_step,
-                                     jnp.zeros((tile, tile), jnp.float32), unroll=True))
-        gate_pre, up_pre = pre
+        panels = [panel_ref[m, f * per_block:(f + 1) * per_block].reshape(per_block * tile, tile)
+                  for m in range(2)]
+        gate_pre, up_pre = [jnp.dot(picked_ref[m], panels[m], preferred_element_type=jnp.float32)
+                            for m in range(2)]
         cols = slice(f * tile, (f + 1) * tile)
         hg = hgrad_ref[:, cols].astype(jnp.float32)
         sig = 1.0 / (1.0 + jnp.exp(-gate_pre))
@@ -76,17 +75,15 @@
         up_delta = (hg * gate_pre * sig).astype(jnp.bfloat16)
         for m, delta in ((0, gate_delta), (1, up_delta)):
             delta_t = delta.astype(jnp.float32).T.astype(jnp.bfloat16)
-            for k in range(per_block):
-                r = rows_ref[m, f * per_block + k]
-                picked_ref[k * tile:(k + 1) * tile, :] = tokt_ref[r]
-            panel = panel_ref[m, f * per_block:(f + 1) * per_block].reshape(per_block * tile, tile)
-            back_t = jnp.dot(panel, delta_t, preferred_element_type=jnp.float32)
-            term = jnp.dot(picked_ref[...], delta, preferred_element_type=jnp.float32)
+            back = lax.dot_general(delta, panels[m], (((1,), (1,)), ((), ())),
+                                   preferred_element_type=jnp.float32)
+            term_t = jnp.dot(delta_t, picked_ref[m], preferred_element_type=jnp.float32)
             for k in range(per_block):
                 i = f * per_block + k
                 r = rows_ref[m, i]
-                acc_ref[r] = acc_ref[r] + back_t[k * tile:(k + 1) * tile]
-                term_ref[m, i] = term[k * tile:(k + 1) * tile].astype(term_ref.dtype)
+                blk = slice(k * tile, (k + 1) * tile)
+                acc_ref[r] = acc_ref[r] + back[:, blk]
+                term_ref[m, i] = term_t[:, blk].astype(term_ref.dtype)
                 tile_copy_out(m, i).start()
     tpart_ref[...] = acc_ref[...].astype(tpart_ref.dtype)
 
@@ -103,34 +100,35 @@
     lax.fori_loop(0, free_count, wait_zero, 0)
 
 
-def swiglu_local(rows, slots, free, tok_bm, tokt_bm, store, hgrad, interpret=False):
+def swiglu_local(rows, slots, free, tok_bm, store, hgrad, interpret=False):
     row_blocks, tok_count, tile = tok_bm.shape
     tile_count = rows.shape[1]
     free_count = free.shape[1]
+    per_block = tile_count // (hgrad.shape[1] // tile)
     smem = pl.BlockSpec(memory_space=pltpu.SMEM)
     vmem = pl.BlockSpec(memory_space=pltpu.VMEM)
     hbm = pl.BlockSpec(memory_space=pl.ANY)
     out_shape = (
         jax.ShapeDtypeStruct(hgrad.shape, jnp.bfloat16),
-        jax.ShapeDtypeStruct((row_blocks, tile, tok_count), jnp.bfloat16),
+        jax.ShapeDtypeStruct((row_blocks, tok_count, tile), jnp.bfloat16),
         jax.ShapeDtypeStruct(store.shape, jnp.bfloat16),
     )
     return pl.pallas_call(
         _swiglu_kernel,
         out_shape=out_shape,
-        in_specs=[smem, smem, smem, vmem, vmem, hbm, vmem],
+        in_specs=[smem, smem, smem, vmem, hbm, vmem],
         out_specs=(vmem, vmem, hbm),
-        scratch_shapes=[pltpu.VMEM((row_blocks, tile, tok_count), jnp.float32),
+        scratch_shapes=[pltpu.VMEM((row_blocks, tok_count, tile), jnp.float32),
                         pltpu.VMEM((2, tile_count, tile, tile), jnp.bfloat16),
                         pltpu.VMEM((2, tile_count, tile, tile), jnp.bfloat16),
-                        pltpu.VMEM((tile_count // (hgrad.shape[1] // tile) * tile, tok_count), jnp.bfloat16),
+                        pltpu.VMEM((2, tok_count, per_block * tile), jnp.bfloat16),
                         pltpu.VMEM((tile, tile), jnp.bfloat16),
                         pltpu.SemaphoreType.DMA((2 * tile_count,)),
                         pltpu.SemaphoreType.DMA((2 * tile_count,)),
                         pltpu.SemaphoreType.DMA((2 * free_count,))],
         compiler_params=pltpu.CompilerParams(vmem_limit_bytes=100 * 1024 * 1024),
         interpret=interpret,
-    )(rows, slots, free, tok_bm, tokt_bm, store, hgrad)
+    )(rows, slots, free, tok_bm, store, hgrad)
 
 
 def free_slots(slots, slot_total):
@@ -152,7 +150,6 @@
     row_blocks = model_width // tile_size
     tok_blocks = gathered_tok.reshape(tok_count, row_blocks, tile_size)
     tok_bm = tok_blocks.transpose(1, 0, 2)
-    tokt_bm = tok_blocks.transpose(1, 2, 0)
     tile_count = tile_rows.shape[1] * tile_rows.shape[2]
     row_flat = tile_rows.reshape(2, tile_count)
     slot_stack = jnp.stack(
@@ -165,14 +162,16 @@
     local_pair = jnp.stack([gate_tiles[0], up_tiles[0]], axis=1)
     store = lax.all_gather(local_pair, "dp", axis=0, tiled=True)
     free = free_slots(slot_stack, store.shape[0])
-    hidden, tpart_t, grads = swiglu_local(
-        row_flat, slot_stack, free, tok_bm, tokt_bm, store, hidden_grad
-    )
-    token_part = tpart_t.transpose(2, 0, 1).reshape(tok_count, model_width)
+    hidden, tpart_bm, grads_t = swiglu_local(
+        row_flat, slot_stack, free, tok_bm, store, hidden_grad
+    )
+    token_part = tpart_bm.transpose(1, 0, 2).reshape(tok_count, model_width)
     part_rows = token_part.reshape(tensor_count, tok_count // tensor_count, model_width)
     part_recv = lax.all_to_all(part_rows, "tensor", 0, 0, tiled=True)
     token_grad = jnp.sum(part_recv.astype(jnp.float32), axis=0).astype(jnp.bfloat16)
-    tile_sums = lax.psum_scatter(grads, "dp", scatter_dimension=0, tiled=True)
+    tile_sums = lax.psum_scatter(grads_t, "dp", scatter_dimension=0, tiled=True).transpose(
+        0, 1, 3, 2
+    )
     gate_grad = tile_sums[:, 0][None]
     up_grad = tile_sums[:, 1][None]
     return (hidden, token_grad, gate_grad, up_grad)

time: 209 us -> 210 us (level)
  waiting for transfers between devices: 90.1 us -> 96.3 us
  local copies, waits for them, and re-layouts: 31.7 us -> 26.5 us
    all_gather x1, waiting for transfers between devices: 38.5 us -> 44.4 us  [body(): store = lax.all_gather(local_pair, 'dp', axis=0, tiled=True)]
    another operation x2 -> x1, local copies, waits for them, and re-layouts: 5.61 us -> 2.66 us  [body(): tok_blocks = gathered_tok.reshape(tok_count, row_blocks, tile_size)]
  transfers between devices with their start and end apart: 3 -> 3, of which waited for: 3 -> 3; matrix products, arithmetic and copies ran while one was open for 16% -> 14% of each run, Pallas kernels for 0% -> 0%
where the time goes in v5:
time: 210 us; the launch traced here: 209 us
  waiting for transfers between devices  96.3 us (46%)
  blocking collectives  34.7 us (17%)
  local copies, waits for them, and re-layouts  26.5 us (13%)
  Pallas kernels  22.5 us (11%)
  between operations  14.1 us (7%)
  starting transfers between devices  7.68 us (4%)
  other arithmetic  7.41 us (4%)
    all_gather x1, waiting for transfers between devices, body(): store = lax.all_gather(local_pair, 'dp', axis=0, tiled=True)  44.4 us
    reduce_scatter x1, waiting for transfers between devices, body(): lax.psum_scatter(grads_t, 'dp', scatter_dimension=0, tiled=True)  42.5 us
    all_to_all x1, blocking collectives, body(): part_recv = lax.all_to_all(part_rows, 'tensor', 0, 0, tiled=True)  34.7 us
    pallas_call x1, Pallas kernels, swiglu_local(): pl.pallas_call(_swiglu_kernel, out_shape=out_shape, in_specs=[smem, smem,...  22.5 us
    scatter x1, local copies, waits for them, and re-layouts, free_slots(): taken = jnp.zeros((slots.shape[0], slot_total), jnp.int32).at[jnp.arange(...  11.7 us
    all_to_all x1, waiting for transfers between devices, body(): lax.all_to_all(tok_copies, 'tensor', 0, 0, tiled=True)  9.43 us
    all_to_all x1, starting transfers between devices, body(): lax.all_to_all(tok_copies, 'tensor', 0, 0, tiled=True)  7.61 us
  transfers between devices with their start and end apart: 3, of which 3 were waited for; matrix products, arithmetic and copies ran while one was open for 14% of the time, Pallas kernels for 0%

profile of v5, /device:TPU:2, one launch (start us, length us, event | category | flops | bytes accessed | tf_op | source)
XLA Modules:
  0.0 209.2 jit_solution(17393500100458514090)
XLA Ops:
  7.2 2.2 %pad_maximum_fusion = bf16[13,2,128,128]{3,2,1,0:T(8,128)(2,1)} fusion(bf16[13,1,128,128]{3,2,1,0:T(8,128)(2,1)} %bitcast.26, bf16[13,1,128,128]{3,2,1,0:T(8,128)(2,1)} %bitcast.27), kind=kLoop, calls=%fused_computation.2 | loop fusion | flops 425984 | bytes 1703936 | tf_op jit(solution)/shard_map/stack | solution.py:162
  9.4 1.5 broadcast_in_dim.11
  10.9 7.6 %all-to-all-start = ((bf16[16,8,8192]{2,1,0:T(8,128)(2,1)}), bf16[16,8,8192]{2,1,0:T(8,128)(2,1)S(1)}, u32[]{:S(2)}, u32[]{:S(2)}) async-start(bf16[16,8,8192]{2,1,0:T(8,128)(2,1)} %broadcast_in_dim.11), calls=%async_computation | async-start | bytes 4194304 | tf_op jit(solution)/shard_map/all_to_all | solution.py:146
  18.6 0.6 reshape.151.rows_ref
  19.6 0.2 convert_reduce_fusion.1
  19.8 0.2 convert_reduce_fusion
  20.0 0.1 reshape.152
  20.1 11.7 %scatter_fusion = s32[2,208]{1,0:T(2,128)S(1)} fusion(s32[2,208]{1,0:T(2,128)S(1)} %broadcast_in_dim.8, s32[224]{0:T(256)S(1)} %reshape.152, s32[224]{0:T(256)S(1)} %broadcast.81), kind=kCustom, calls=%fused_computation | custom fusion | bytes 4480 | tf_op jit(solution)/shard_map/scatter | solution.py:136
  31.8 3.3 %sort.17 = (s32[2,208]{1,0:T(2,128)}, s32[2,208]{1,0:T(2,128)S(1)}) sort(s32[2,208]{1,0:T(2,128)S(1)} %scatter_fusion, s32[2,208]{1,0:T(2,128)S(1)} %iota.18), dimensions={1}, to_apply=%region_3.0 | sort | flops 3744 | bytes 6656 | tf_op jit(solution)/shard_map/jit(argsort)/sort | solution.py:137
  35.1 0.6 slice.17.free_ref
  35.7 0.6 pad_add_fusion.slots_ref
  36.2 9.4 %all-to-all-done = bf16[16,8,8192]{2,1,0:T(8,128)(2,1)S(1)} async-done(((bf16[16,8,8192]{2,1,0:T(8,128)(2,1)}), bf16[16,8,8192]{2,1,0:T(8,128)(2,1)S(1)}, u32[]{:S(2)}, u32[]{:S(2)}) %all-to-all-start) | async-done | bytes 2097184 | tf_op jit(solution)/shard_map/all_to_all | solution.py:146
  45.7 0.6 copy.28
  46.3 2.7 %copy.30 = bf16[128,64,128]{2,0,1:T(8,128)(2,1)} copy(bf16[128,64,128]{2,1,0:T(8,128)(2,1)S(1)} %bitcast.23) | data formatting | bytes 4194304 | tf_op jit(solution)/shard_map/reshape;reshape | solution.py:151
  48.9 44.4 %all-gather.2.cloned.1.call-done.store_hbm = bf16[208,2,128,128]{3,2,1,0:T(8,128)(2,1)} async-done(((bf16[13,2,128,128]{3,2,1,0:T(8,128)(2,1)}), bf16[208,2,128,128]{3,2,1,0:T(8,128)(2,1)}) %all-gather.2.cloned.1.call-update) | async-done | bytes 13631504 | tf_op jit(solution)/shard_map/all_gather | solution.py:163
  93.3 22.5 %shard_map.93 = (bf16[128,896]{1,0:T(8,128)(2,1)}, bf16[64,128,128]{2,1,0:T(8,128)(2,1)}, bf16[208,2,128,128]{3,2,1,0:T(8,128)(2,1)}) custom-call(s32[2,112]{1,0:T(2,128)} %reshape.151.rows_ref, s32[2,112]{1,0:T(2,128)} %pad_add_fusion.slots_ref, s32[2,96]{1,0:T(2,128)} %slice.17.free_ref, bf16[64,128,128]{2,1,0:T(8,128)(2,1)} %bitcast.21, ...), custom_call_target="tpu_custom_call" | custom-call | tf_op jit(solution)/shard_map/pallas_call | solution.py:116
  115.8 2.9 %copy.25 = bf16[128,64,128]{2,1,0:T(8,128)(2,1)S(1)} copy(bf16[128,64,128]{2,0,1:T(8,128)(2,1)} %bitcast.24) | data formatting | bytes 4194304 | tf_op jit(solution)/shard_map/transpose | solution.py:168
  118.8 2.3 %reshape_reshape.7 = bf16[16,8,8192]{2,1,0:T(8,128)(2,1)} reshape(bf16[128,64,128]{2,1,0:T(8,128)(2,1)S(1)} %copy.25) | data formatting | bytes 4194304 | tf_op jit(solution)/shard_map/reshape;reshape | solution.py:169
  121.1 34.7 %all_to_all.10 = bf16[16,8,8192]{2,1,0:T(8,128)(2,1)S(1)} all-to-all(bf16[16,8,8192]{2,1,0:T(8,128)(2,1)} %reshape_reshape.7), channel_id=1, replica_groups=mesh['dp'=16,'tensor'=16] {'tensor'}, dimensions={0} | all-to-all | bytes 4194304 | tf_op jit(solution)/shard_map/all_to_all | solution.py:170
  155.8 1.0 reduce_sum.38
  156.8 42.5 %reduce-scatter.2.cloned.1.call-done = bf16[13,2,128,128]{3,2,1,0:T(8,128)(2,1)} async-done(((bf16[208,2,128,128]{3,2,1,0:T(8,128)(2,1)}), bf16[13,2,128,128]{3,2,1,0:T(8,128)(2,1)}) %reduce-scatter.2.cloned.1.call-update) | async-done | bytes 851984 | tf_op jit(solution)/shard_map/reduce_scatter | solution.py:172
  199.3 1.2 slice_bitcast_fusion
  200.5 1.0 copy.27
  201.4 1.0 copy.26
  (21 shorter events, 0.5 us)
Async XLA Ops:
  7.2 2.3 %copy-start = (bf16[8,8192]{1,0:T(8,128)(2,1)S(1)}, bf16[8,8192]{1,0:T(8,128)(2,1)}, u32[]{:S(2)}) copy-start(bf16[8,8192]{1,0:T(8,128)(2,1)} %param.6) | copy-start | bytes 393220
  7.2 86.2 %all-gather.2.cloned.1.call-start = ((), (), s32[]{:S(2)}) async-start(), calls=%async_computation.3 | async-start | bytes 14483456 | tf_op jit(solution)/shard_map/all_gather | solution.py:163
  10.9 7.7 %copy-start.1 = (s32[2,7,16]{2,0,1:T(2,128)S(1)}, s32[2,7,16]{2,0,1:T(2,128)}, u32[]{:S(2)}) copy-start(s32[2,7,16]{2,0,1:T(2,128)} %param.10) | copy-start | bytes 2692
  10.9 8.3 %copy-start.2 = (s32[2,7,16]{2,0,1:T(2,128)S(1)}, s32[2,7,16]{2,0,1:T(2,128)}, u32[]{:S(2)}) copy-start(s32[2,7,16]{2,0,1:T(2,128)} %param.11) | copy-start | bytes 2692
  10.9 34.7 %all-to-all-start = ((bf16[16,8,8192]{2,1,0:T(8,128)(2,1)}), bf16[16,8,8192]{2,1,0:T(8,128)(2,1)S(1)}, u32[]{:S(2)}, u32[]{:S(2)}) async-start(bf16[16,8,8192]{2,1,0:T(8,128)(2,1)} %broadcast_in_dim.11), calls=%async_computation | async-start | bytes 4194304 | tf_op jit(solution)/shard_map/all_to_all | solution.py:146
  18.5 180.7 %reduce-scatter.2.cloned.1.call-start = ((), (), s32[]{:S(2)}) async-start(), calls=%async_computation.4 | async-start | bytes 14483456 | tf_op jit(solution)/shard_map/reduce_scatter | solution.py:172
Sparse Core Ops, SparseCore 0:
  9.8 83.4 all-gather.1
  116.0 83.2 reduce-scatter.1

commit v6 on v2

v6 whole, which is shorter than its diff:
```python
import jax
import jax.numpy as jnp
from jax import lax
from jax.experimental import pallas as pl
from jax.experimental.pallas import tpu as pltpu
from jax.sharding import PartitionSpec as P


def slot_index(owner_ids, capacity):
    tile_total = owner_ids.shape[0]
    tile_order = jnp.arange(tile_total, dtype=jnp.int32)
    same_owner = (owner_ids[:, None] == owner_ids[None, :]) & (
        tile_order[None, :] < tile_order[:, None]
    )
    tile_ranks = jnp.sum(same_owner.astype(jnp.int32), axis=1)
    return owner_ids * capacity + tile_ranks


def _swiglu_kernel(rows_ref, slots_ref, tok_ref, store_ref, hgrad_ref,
                   hidden_ref, tpart_ref, grad_ref, acc_ref, panel_ref, picked_ref):
    group_blocks = hgrad_ref.shape[1] // 128
    tile_count = rows_ref.shape[1]
    per_block = tile_count // group_blocks
    tile = store_ref.shape[2]
    acc_ref[...] = jnp.zeros(acc_ref.shape, jnp.float32)
    grad_ref[...] = jnp.zeros(grad_ref.shape, grad_ref.dtype)
    for f in range(group_blocks):
        for m in range(2):
            for k in range(per_block):
                i = f * per_block + k
                r = rows_ref[m, i]
                s = slots_ref[m, i]
                blk = slice(k * tile, (k + 1) * tile)
                picked_ref[m, :, blk] = tok_ref[r]
                panel_ref[m, blk, :] = store_ref[s, m]
        gate_pre, up_pre = [jnp.dot(picked_ref[m], panel_ref[m], preferred_element_type=jnp.float32)
                            for m in range(2)]
        cols = slice(f * tile, (f + 1) * tile)
        hg = hgrad_ref[:, cols].astype(jnp.float32)
        sig = 1.0 / (1.0 + jnp.exp(-gate_pre))
        hidden_ref[:, cols] = (gate_pre * sig * up_pre).astype(hidden_ref.dtype)
        gate_delta = (hg * up_pre * sig * (1.0 + gate_pre * (1.0 - sig))).astype(jnp.bfloat16)
        up_delta = (hg * gate_pre * sig).astype(jnp.bfloat16)
        for m, delta in ((0, gate_delta), (1, up_delta)):
            delta_t = delta.astype(jnp.float32).T.astype(jnp.bfloat16)
            back = lax.dot_general(delta, panel_ref[m], (((1,), (1,)), ((), ())),
                                   preferred_element_type=jnp.float32)
            term_t = jnp.dot(delta_t, picked_ref[m], preferred_element_type=jnp.float32)
            for k in range(per_block):
                i = f * per_block + k
                r = rows_ref[m, i]
                s = slots_ref[m, i]
                blk = slice(k * tile, (k + 1) * tile)
                acc_ref[r] = acc_ref[r] + back[:, blk]
                grad_ref[s, m] = term_t[:, blk].astype(grad_ref.dtype)
    tpart_ref[...] = acc_ref[...].astype(tpart_ref.dtype)


def swiglu_local(rows, slots, tok_bm, store, hgrad, interpret=False):
    row_blocks, tok_count, tile = tok_bm.shape
    tile_count = rows.shape[1]
    per_block = tile_count // (hgrad.shape[1] // tile)
    smem = pl.BlockSpec(memory_space=pltpu.SMEM)
    vmem = pl.BlockSpec(memory_space=pltpu.VMEM)
    out_shape = (
        jax.ShapeDtypeStruct(hgrad.shape, jnp.bfloat16),
        jax.ShapeDtypeStruct((row_blocks, tok_count, tile), jnp.bfloat16),
        jax.ShapeDtypeStruct(store.shape, jnp.bfloat16),
    )
    return pl.pallas_call(
        _swiglu_kernel,
        out_shape=out_shape,
        in_specs=[smem, smem, vmem, vmem, vmem],
        out_specs=(vmem, vmem, vmem),
        scratch_shapes=[pltpu.VMEM((row_blocks, tok_count, tile), jnp.float32),
                        pltpu.VMEM((2, per_block * tile, tile), jnp.bfloat16),
                        pltpu.VMEM((2, tok_count, per_block * tile), jnp.bfloat16)],
        compiler_params=pltpu.CompilerParams(vmem_limit_bytes=100 * 1024 * 1024),
        interpret=interpret,
    )(rows, slots, tok_bm, store, hgrad)


def body(tokens, hidden_grad, gate_tiles, up_tiles, tile_rows, tile_owner):
    tile_size = gate_tiles.shape[2]
    capacity = gate_tiles.shape[1]
    tensor_count = lax.axis_size("tensor")
    tok_copies = jnp.broadcast_to(tokens[None], (tensor_count,) + tokens.shape)
    gathered_tok = lax.all_to_all(tok_copies, "tensor", 0, 0, tiled=True).reshape(
        tensor_count * tokens.shape[0], tokens.shape[1]
    )
    tok_count, model_width = gathered_tok.shape
    row_blocks = model_width // tile_size
    tok_blocks = gathered_tok.reshape(tok_count, row_blocks, tile_size)
    tok_bm = tok_blocks.transpose(1, 0, 2)
    tile_count = tile_rows.shape[1] * tile_rows.shape[2]
    row_flat = tile_rows.reshape(2, tile_count)
    slot_stack = jnp.stack(
        [
            slot_index(tile_owner[0].reshape(-1), capacity),
            slot_index(tile_owner[1].reshape(-1), capacity),
        ],
        axis=0,
    )
    local_pair = jnp.stack([gate_tiles[0], up_tiles[0]], axis=1)
    store = lax.all_gather(local_pair, "dp", axis=0, tiled=True)
    hidden, tpart_bm, grads_t = swiglu_local(row_flat, slot_stack, tok_bm, store, hidden_grad)
    token_part = tpart_bm.transpose(1, 0, 2).reshape(tok_count, model_width)
    part_rows = token_part.reshape(tensor_count, tok_count // tensor_count, model_width)
    part_recv = lax.all_to_all(part_rows, "tensor", 0, 0, tiled=True)
    token_grad = jnp.sum(part_recv.astype(jnp.float32), axis=0).astype(jnp.bfloat16)
    tile_sums = lax.psum_scatter(grads_t, "dp", scatter_dimension=0, tiled=True).transpose(
        0, 1, 3, 2
    )
    gate_grad = tile_sums[:, 0][None]
    up_grad = tile_sums[:, 1][None]
    return (hidden, token_grad, gate_grad, up_grad)


def solution(mesh):
    placed = (
        P(("dp", "tensor"), None),
        P("dp", "tensor"),
        P("tensor", "dp", None, None),
        P("tensor", "dp", None, None),
        P(None, "tensor", None),
        P(None, "tensor", None),
    )
    return jax.shard_map(
        body,
        mesh=mesh,
        in_specs=placed,
        out_specs=(
            P("dp", "tensor"),
            P(("dp", "tensor"), None),
            P("tensor", "dp", None, None),
            P("tensor", "dp", None, None),
        ),
        check_vma=False,
    )
```

time: 211 us -> 208 us (0.986)
  waiting for transfers between devices: 106 us -> 112 us
  local copies, waits for them, and re-layouts: 19 us -> 14.1 us
  Pallas kernels: 24.9 us -> 21.1 us
    all_gather x1, waiting for transfers between devices: 38.5 us -> 44.4 us  [body(): store = lax.all_gather(local_pair, 'dp', axis=0, tiled=True)]
    pallas_call x1, Pallas kernels: 24.9 us -> 21.1 us  [swiglu_local(): pl.pallas_call(_swiglu_kernel, out_shape=out_shape, in_specs=[smem, smem,...]
    another operation x2 -> x1, local copies, waits for them, and re-layouts: 5.61 us -> 2.66 us  [body(): tok_blocks = gathered_tok.reshape(tok_count, row_blocks, tile_size)]
  transfers between devices with their start and end apart: 3 -> 3, of which waited for: 3 -> 3; matrix products, arithmetic and copies ran while one was open for 8% -> 6% of each run, Pallas kernels for 0% -> 0%
where the time goes in v6:
time: 208 us
  waiting for transfers between devices  112 us (54%)
  blocking collectives  34.7 us (17%)
  Pallas kernels  21.1 us (10%)
  local copies, waits for them, and re-layouts  14.1 us (7%)
  between operations  14.1 us (7%)
  starting transfers between devices  7.68 us (4%)
  other arithmetic  4.12 us (2%)
    all_gather x1, waiting for transfers between devices, body(): store = lax.all_gather(local_pair, 'dp', axis=0, tiled=True)  44.4 us
    reduce_scatter x1, waiting for transfers between devices, body(): lax.psum_scatter(grads_t, 'dp', scatter_dimension=0, tiled=True)  42.5 us
    all_to_all x1, blocking collectives, body(): part_recv = lax.all_to_all(part_rows, 'tensor', 0, 0, tiled=True)  34.7 us
    all_to_all x1, waiting for transfers between devices, body(): lax.all_to_all(tok_copies, 'tensor', 0, 0, tiled=True)  25.1 us
    pallas_call x1, Pallas kernels, swiglu_local(): pl.pallas_call(_swiglu_kernel, out_shape=out_shape, in_specs=[smem, smem,...  21.1 us
    all_to_all x1, starting transfers between devices, body(): lax.all_to_all(tok_copies, 'tensor', 0, 0, tiled=True)  7.61 us
  transfers between devices with their start and end apart: 3, of which 3 were waited for; matrix products, arithmetic and copies ran while one was open for 6% of the time, Pallas kernels for 0%

profile of v6, /device:TPU:2, one launch (start us, length us, event | category | flops | bytes accessed | tf_op | source)
XLA Modules:
  0.0 207.8 jit_solution(14949100997044049542)
XLA Ops:
  7.2 2.2 %pad_maximum_fusion = bf16[13,2,128,128]{3,2,1,0:T(8,128)(2,1)} fusion(bf16[13,1,128,128]{3,2,1,0:T(8,128)(2,1)} %bitcast.23, bf16[13,1,128,128]{3,2,1,0:T(8,128)(2,1)} %bitcast.24), kind=kLoop, calls=%fused_computation.1 | loop fusion | flops 425984 | bytes 1703936 | tf_op jit(solution)/shard_map/stack | solution.py:104
  9.4 1.5 broadcast_in_dim.2
  10.9 7.6 %all-to-all-start = ((bf16[16,8,8192]{2,1,0:T(8,128)(2,1)}), bf16[16,8,8192]{2,1,0:T(8,128)(2,1)S(1)}, u32[]{:S(2)}, u32[]{:S(2)}) async-start(bf16[16,8,8192]{2,1,0:T(8,128)(2,1)} %broadcast_in_dim.2), calls=%async_computation | async-start | bytes 4194304 | tf_op jit(solution)/shard_map/all_to_all | solution.py:88
  18.6 0.6 reshape.54.rows_ref
  19.3 0.1 eq.30
  19.4 0.1 eq.34
  19.5 0.1 mul.29
  19.5 0.1 mul.27
  19.6 0.2 convert_reduce_fusion.1
  19.8 0.2 convert_reduce_fusion
  20.0 0.6 pad_add_fusion.slots_ref
  20.6 25.1 %all-to-all-done = bf16[16,8,8192]{2,1,0:T(8,128)(2,1)S(1)} async-done(((bf16[16,8,8192]{2,1,0:T(8,128)(2,1)}), bf16[16,8,8192]{2,1,0:T(8,128)(2,1)S(1)}, u32[]{:S(2)}, u32[]{:S(2)}) %all-to-all-start) | async-done | bytes 2097184 | tf_op jit(solution)/shard_map/all_to_all | solution.py:88
  45.7 0.6 copy.28
  46.3 2.7 %copy.30 = bf16[128,64,128]{2,0,1:T(8,128)(2,1)} copy(bf16[128,64,128]{2,1,0:T(8,128)(2,1)S(1)} %bitcast.20) | data formatting | bytes 4194304 | tf_op jit(solution)/shard_map/reshape;reshape | solution.py:93
  48.9 44.4 %all-gather.2.cloned.1.call-done.store_ref = bf16[208,2,128,128]{3,2,1,0:T(8,128)(2,1)} async-done(((bf16[13,2,128,128]{3,2,1,0:T(8,128)(2,1)}), bf16[208,2,128,128]{3,2,1,0:T(8,128)(2,1)}) %all-gather.2.cloned.1.call-update) | async-done | bytes 13631504 | tf_op jit(solution)/shard_map/all_gather | solution.py:105
  93.3 21.1 %shard_map.93 = (bf16[128,896]{1,0:T(8,128)(2,1)}, bf16[64,128,128]{2,1,0:T(8,128)(2,1)}, bf16[208,2,128,128]{3,2,1,0:T(8,128)(2,1)}) custom-call(s32[2,112]{1,0:T(2,128)} %reshape.54.rows_ref, s32[2,112]{1,0:T(2,128)} %pad_add_fusion.slots_ref, bf16[64,128,128]{2,1,0:T(8,128)(2,1)} %bitcast.18, ...), custom_call_target="tpu_custom_call" | custom-call | tf_op jit(solution)/shard_map/pallas_call | solution.py:70
  114.4 2.9 %copy.25 = bf16[128,64,128]{2,1,0:T(8,128)(2,1)S(1)} copy(bf16[128,64,128]{2,0,1:T(8,128)(2,1)} %bitcast.21) | data formatting | bytes 4194304 | tf_op jit(solution)/shard_map/transpose | solution.py:107
  117.4 2.3 %reshape_reshape.7 = bf16[16,8,8192]{2,1,0:T(8,128)(2,1)} reshape(bf16[128,64,128]{2,1,0:T(8,128)(2,1)S(1)} %copy.25) | data formatting | bytes 4194304 | tf_op jit(solution)/shard_map/reshape;reshape | solution.py:108
  119.7 34.7 %all_to_all.10 = bf16[16,8,8192]{2,1,0:T(8,128)(2,1)S(1)} all-to-all(bf16[16,8,8192]{2,1,0:T(8,128)(2,1)} %reshape_reshape.7), channel_id=1, replica_groups=mesh['dp'=16,'tensor'=16] {'tensor'}, dimensions={0} | all-to-all | bytes 4194304 | tf_op jit(solution)/shard_map/all_to_all | solution.py:109
  154.4 1.0 reduce_sum.38
  155.4 42.5 %reduce-scatter.2.cloned.1.call-done = bf16[13,2,128,128]{3,2,1,0:T(8,128)(2,1)} async-done(((bf16[208,2,128,128]{3,2,1,0:T(8,128)(2,1)}), bf16[13,2,128,128]{3,2,1,0:T(8,128)(2,1)}) %reduce-scatter.2.cloned.1.call-update) | async-done | bytes 851984 | tf_op jit(solution)/shard_map/reduce_scatter | solution.py:111
  197.8 1.2 slice_bitcast_fusion
  199.0 1.0 copy.27
  200.0 1.0 copy.26
  (13 shorter events, 0.2 us)
Async XLA Ops:
  7.2 2.3 %copy-start = (bf16[8,8192]{1,0:T(8,128)(2,1)S(1)}, bf16[8,8192]{1,0:T(8,128)(2,1)}, u32[]{:S(2)}) copy-start(bf16[8,8192]{1,0:T(8,128)(2,1)} %param.6) | copy-start | bytes 393220
  7.2 86.1 %all-gather.2.cloned.1.call-start = ((), (), s32[]{:S(2)}) async-start(), calls=%async_computation.3 | async-start | bytes 14483456 | tf_op jit(solution)/shard_map/all_gather | solution.py:105
  10.9 7.7 %copy-start.1 = (s32[2,7,16]{2,0,1:T(2,128)S(1)}, s32[2,7,16]{2,0,1:T(2,128)}, u32[]{:S(2)}) copy-start(s32[2,7,16]{2,0,1:T(2,128)} %param.10) | copy-start | bytes 2692
  10.9 8.3 %copy-start.2 = (s32[2,7,16]{2,0,1:T(2,128)S(1)}, s32[2,7,16]{2,0,1:T(2,128)}, u32[]{:S(2)}) copy-start(s32[2,7,16]{2,0,1:T(2,128)} %param.11) | copy-start | bytes 2692
  10.9 34.7 %all-to-all-start = ((bf16[16,8,8192]{2,1,0:T(8,128)(2,1)}), bf16[16,8,8192]{2,1,0:T(8,128)(2,1)S(1)}, u32[]{:S(2)}, u32[]{:S(2)}) async-start(bf16[16,8,8192]{2,1,0:T(8,128)(2,1)} %broadcast_in_dim.2), calls=%async_computation | async-start | bytes 4194304 | tf_op jit(solution)/shard_map/all_to_all | solution.py:88
  18.5 179.3 %reduce-scatter.2.cloned.1.call-start = ((), (), s32[]{:S(2)}) async-start(), calls=%async_computation.4 | async-start | bytes 14483456 | tf_op jit(solution)/shard_map/reduce_scatter | solution.py:111
Sparse Core Ops, SparseCore 0:
  9.8 83.4 all-gather.1
  114.5 83.2 reduce-scatter.1

commit v7 on v6

--- a/solution.py
+++ b/solution.py
@@ -16,14 +16,18 @@
     return owner_ids * capacity + tile_ranks
 
 
-def _swiglu_kernel(rows_ref, slots_ref, tok_ref, store_ref, hgrad_ref,
-                   hidden_ref, tpart_ref, grad_ref, acc_ref, panel_ref, picked_ref):
+def _swiglu_kernel(rows_ref, slots_ref, tok_ref, store_hbm, hgrad_ref,
+                   hidden_ref, tpart_ref, grad_ref, acc_ref, panel_ref, picked_ref,
+                   store_ref, store_sem):
     group_blocks = hgrad_ref.shape[1] // 128
     tile_count = rows_ref.shape[1]
     per_block = tile_count // group_blocks
     tile = store_ref.shape[2]
+    store_copy = pltpu.make_async_copy(store_hbm, store_ref, store_sem)
+    store_copy.start()
     acc_ref[...] = jnp.zeros(acc_ref.shape, jnp.float32)
     grad_ref[...] = jnp.zeros(grad_ref.shape, grad_ref.dtype)
+    store_copy.wait()
     for f in range(group_blocks):
         for m in range(2):
             for k in range(per_block):
@@ -70,11 +74,13 @@
     return pl.pallas_call(
         _swiglu_kernel,
         out_shape=out_shape,
-        in_specs=[smem, smem, vmem, vmem, vmem],
+        in_specs=[smem, smem, vmem, pl.BlockSpec(memory_space=pl.ANY), vmem],
         out_specs=(vmem, vmem, vmem),
         scratch_shapes=[pltpu.VMEM((row_blocks, tok_count, tile), jnp.float32),
                         pltpu.VMEM((2, per_block * tile, tile), jnp.bfloat16),
-                        pltpu.VMEM((2, tok_count, per_block * tile), jnp.bfloat16)],
+                        pltpu.VMEM((2, tok_count, per_block * tile), jnp.bfloat16),
+                        pltpu.VMEM(store.shape, jnp.bfloat16),
+                        pltpu.SemaphoreType.DMA(())],
         compiler_params=pltpu.CompilerParams(vmem_limit_bytes=100 * 1024 * 1024),
         interpret=interpret,
     )(rows, slots, tok_bm, store, hgrad)

time: 208 us -> 207 us (level)
  no operation moved by 1% of the time
where the time goes in v7:
time: 207 us
  waiting for transfers between devices  112 us (54%)
  blocking collectives  34.7 us (17%)
  Pallas kernels  20.2 us (10%)
  local copies, waits for them, and re-layouts  14.1 us (7%)
  between operations  14.1 us (7%)
  starting transfers between devices  7.68 us (4%)
  other arithmetic  4.12 us (2%)
    all_gather x1, waiting for transfers between devices, body(): store = lax.all_gather(local_pair, 'dp', axis=0, tiled=True)  44.4 us
    reduce_scatter x1, waiting for transfers between devices, body(): lax.psum_scatter(grads_t, 'dp', scatter_dimension=0, tiled=True)  42.5 us
    all_to_all x1, blocking collectives, body(): part_recv = lax.all_to_all(part_rows, 'tensor', 0, 0, tiled=True)  34.7 us
    all_to_all x1, waiting for transfers between devices, body(): lax.all_to_all(tok_copies, 'tensor', 0, 0, tiled=True)  25.1 us
    pallas_call x1, Pallas kernels, swiglu_local(): pl.pallas_call(_swiglu_kernel, out_shape=out_shape, in_specs=[smem, smem,...  20.2 us
    all_to_all x1, starting transfers between devices, body(): lax.all_to_all(tok_copies, 'tensor', 0, 0, tiled=True)  7.61 us
  transfers between devices with their start and end apart: 3, of which 3 were waited for; matrix products, arithmetic and copies ran while one was open for 6% of the time, Pallas kernels for 0%

profile of v7, /device:TPU:2, one launch (start us, length us, event | category | flops | bytes accessed | tf_op | source)
XLA Modules:
  0.0 207.0 jit_solution(6872509226608680524)
XLA Ops:
  7.2 2.2 %pad_maximum_fusion = bf16[13,2,128,128]{3,2,1,0:T(8,128)(2,1)} fusion(bf16[13,1,128,128]{3,2,1,0:T(8,128)(2,1)} %bitcast.23, bf16[13,1,128,128]{3,2,1,0:T(8,128)(2,1)} %bitcast.24), kind=kLoop, calls=%fused_computation.1 | loop fusion | flops 425984 | bytes 1703936 | tf_op jit(solution)/shard_map/stack | solution.py:110
  9.4 1.5 broadcast_in_dim.2
  10.9 7.6 %all-to-all-start = ((bf16[16,8,8192]{2,1,0:T(8,128)(2,1)}), bf16[16,8,8192]{2,1,0:T(8,128)(2,1)S(1)}, u32[]{:S(2)}, u32[]{:S(2)}) async-start(bf16[16,8,8192]{2,1,0:T(8,128)(2,1)} %broadcast_in_dim.2), calls=%async_computation | async-start | bytes 4194304 | tf_op jit(solution)/shard_map/all_to_all | solution.py:94
  18.6 0.6 reshape.54.rows_ref
  19.3 0.1 eq.30
  19.4 0.1 eq.34
  19.5 0.1 mul.29
  19.5 0.1 mul.27
  19.6 0.2 convert_reduce_fusion.1
  19.8 0.2 convert_reduce_fusion
  20.0 0.6 pad_add_fusion.slots_ref
  20.6 25.1 %all-to-all-done = bf16[16,8,8192]{2,1,0:T(8,128)(2,1)S(1)} async-done(((bf16[16,8,8192]{2,1,0:T(8,128)(2,1)}), bf16[16,8,8192]{2,1,0:T(8,128)(2,1)S(1)}, u32[]{:S(2)}, u32[]{:S(2)}) %all-to-all-start) | async-done | bytes 2097184 | tf_op jit(solution)/shard_map/all_to_all | solution.py:94
  45.7 0.6 copy.28
  46.3 2.7 %copy.30 = bf16[128,64,128]{2,0,1:T(8,128)(2,1)} copy(bf16[128,64,128]{2,1,0:T(8,128)(2,1)S(1)} %bitcast.20) | data formatting | bytes 4194304 | tf_op jit(solution)/shard_map/reshape;reshape | solution.py:99
  48.9 44.4 %all-gather.2.cloned.1.call-done.store_hbm = bf16[208,2,128,128]{3,2,1,0:T(8,128)(2,1)} async-done(((bf16[13,2,128,128]{3,2,1,0:T(8,128)(2,1)}), bf16[208,2,128,128]{3,2,1,0:T(8,128)(2,1)}) %all-gather.2.cloned.1.call-update) | async-done | bytes 13631504 | tf_op jit(solution)/shard_map/all_gather | solution.py:111
  93.3 20.2 %shard_map.93 = (bf16[128,896]{1,0:T(8,128)(2,1)}, bf16[64,128,128]{2,1,0:T(8,128)(2,1)}, bf16[208,2,128,128]{3,2,1,0:T(8,128)(2,1)}) custom-call(s32[2,112]{1,0:T(2,128)} %reshape.54.rows_ref, s32[2,112]{1,0:T(2,128)} %pad_add_fusion.slots_ref, bf16[64,128,128]{2,1,0:T(8,128)(2,1)} %bitcast.18, ...), custom_call_target="tpu_custom_call" | custom-call | tf_op jit(solution)/shard_map/pallas_call | solution.py:74
  113.6 2.9 %copy.25 = bf16[128,64,128]{2,1,0:T(8,128)(2,1)S(1)} copy(bf16[128,64,128]{2,0,1:T(8,128)(2,1)} %bitcast.21) | data formatting | bytes 4194304 | tf_op jit(solution)/shard_map/transpose | solution.py:113
  116.5 2.3 %reshape_reshape.7 = bf16[16,8,8192]{2,1,0:T(8,128)(2,1)} reshape(bf16[128,64,128]{2,1,0:T(8,128)(2,1)S(1)} %copy.25) | data formatting | bytes 4194304 | tf_op jit(solution)/shard_map/reshape;reshape | solution.py:114
  118.9 34.7 %all_to_all.10 = bf16[16,8,8192]{2,1,0:T(8,128)(2,1)S(1)} all-to-all(bf16[16,8,8192]{2,1,0:T(8,128)(2,1)} %reshape_reshape.7), channel_id=1, replica_groups=mesh['dp'=16,'tensor'=16] {'tensor'}, dimensions={0} | all-to-all | bytes 4194304 | tf_op jit(solution)/shard_map/all_to_all | solution.py:115
  153.6 1.0 reduce_sum.38
  154.5 42.5 %reduce-scatter.2.cloned.1.call-done = bf16[13,2,128,128]{3,2,1,0:T(8,128)(2,1)} async-done(((bf16[208,2,128,128]{3,2,1,0:T(8,128)(2,1)}), bf16[13,2,128,128]{3,2,1,0:T(8,128)(2,1)}) %reduce-scatter.2.cloned.1.call-update) | async-done | bytes 851984 | tf_op jit(solution)/shard_map/reduce_scatter | solution.py:117
  197.0 1.2 slice_bitcast_fusion
  198.2 1.0 copy.27
  199.2 1.0 copy.26
  (13 shorter events, 0.2 us)
Async XLA Ops:
  7.2 2.3 %copy-start = (bf16[8,8192]{1,0:T(8,128)(2,1)S(1)}, bf16[8,8192]{1,0:T(8,128)(2,1)}, u32[]{:S(2)}) copy-start(bf16[8,8192]{1,0:T(8,128)(2,1)} %param.6) | copy-start | bytes 393220
  7.2 86.1 %all-gather.2.cloned.1.call-start = ((), (), s32[]{:S(2)}) async-start(), calls=%async_computation.3 | async-start | bytes 14483456 | tf_op jit(solution)/shard_map/all_gather | solution.py:111
  10.9 7.7 %copy-start.1 = (s32[2,7,16]{2,0,1:T(2,128)S(1)}, s32[2,7,16]{2,0,1:T(2,128)}, u32[]{:S(2)}) copy-start(s32[2,7,16]{2,0,1:T(2,128)} %param.10) | copy-start | bytes 2692
  10.9 8.3 %copy-start.2 = (s32[2,7,16]{2,0,1:T(2,128)S(1)}, s32[2,7,16]{2,0,1:T(2,128)}, u32[]{:S(2)}) copy-start(s32[2,7,16]{2,0,1:T(2,128)} %param.11) | copy-start | bytes 2692
  10.9 34.7 %all-to-all-start = ((bf16[16,8,8192]{2,1,0:T(8,128)(2,1)}), bf16[16,8,8192]{2,1,0:T(8,128)(2,1)S(1)}, u32[]{:S(2)}, u32[]{:S(2)}) async-start(bf16[16,8,8192]{2,1,0:T(8,128)(2,1)} %broadcast_in_dim.2), calls=%async_computation | async-start | bytes 4194304 | tf_op jit(solution)/shard_map/all_to_all | solution.py:94
  18.5 178.4 %reduce-scatter.2.cloned.1.call-start = ((), (), s32[]{:S(2)}) async-start(), calls=%async_computation.4 | async-start | bytes 14483456 | tf_op jit(solution)/shard_map/reduce_scatter | solution.py:117
Sparse Core Ops, SparseCore 0:
  9.8 83.4 all-gather.1
  113.7 83.2 reduce-scatter.1

commit v8 on v7

--- a/solution.py
+++ b/solution.py
@@ -16,8 +16,8 @@
     return owner_ids * capacity + tile_ranks
 
 
-def _swiglu_kernel(rows_ref, slots_ref, tok_ref, store_hbm, hgrad_ref,
-                   hidden_ref, tpart_ref, grad_ref, acc_ref, panel_ref, picked_ref,
+def _swiglu_kernel(rows_ref, slots_ref, near_ref, far_ref, tok_ref, store_hbm, rest_ref,
+                   hgrad_ref, hidden_ref, tpart_ref, grad_ref, acc_ref, panel_ref, picked_ref,
                    store_ref, store_sem):
     group_blocks = hgrad_ref.shape[1] // 128
     tile_count = rows_ref.shape[1]
@@ -33,10 +33,18 @@
             for k in range(per_block):
                 i = f * per_block + k
                 r = rows_ref[m, i]
-                s = slots_ref[m, i]
                 blk = slice(k * tile, (k + 1) * tile)
+                near = near_ref[m, i]
+                far = far_ref[m, i]
                 picked_ref[m, :, blk] = tok_ref[r]
-                panel_ref[m, blk, :] = store_ref[s, m]
+
+                @pl.when(far < 0)
+                def _(m=m, blk=blk, near=near):
+                    panel_ref[m, blk, :] = store_ref[near, m]
+
+                @pl.when(far >= 0)
+                def _(m=m, blk=blk, far=far):
+                    panel_ref[m, blk, :] = rest_ref[far, m]
         gate_pre, up_pre = [jnp.dot(picked_ref[m], panel_ref[m], preferred_element_type=jnp.float32)
                             for m in range(2)]
         cols = slice(f * tile, (f + 1) * tile)
@@ -60,8 +68,9 @@
     tpart_ref[...] = acc_ref[...].astype(tpart_ref.dtype)
 
 
-def swiglu_local(rows, slots, tok_bm, store, hgrad, interpret=False):
+def swiglu_local(rows, slots, near, far, tok_bm, store, rest, hgrad, interpret=False):
     row_blocks, tok_count, tile = tok_bm.shape
+    slot_total = store.shape[0] + rest.shape[0]
     tile_count = rows.shape[1]
     per_block = tile_count // (hgrad.shape[1] // tile)
     smem = pl.BlockSpec(memory_space=pltpu.SMEM)
@@ -69,12 +78,12 @@
     out_shape = (
         jax.ShapeDtypeStruct(hgrad.shape, jnp.bfloat16),
         jax.ShapeDtypeStruct((row_blocks, tok_count, tile), jnp.bfloat16),
-        jax.ShapeDtypeStruct(store.shape, jnp.bfloat16),
+        jax.ShapeDtypeStruct((slot_total,) + store.shape[1:], jnp.bfloat16),
     )
     return pl.pallas_call(
         _swiglu_kernel,
         out_shape=out_shape,
-        in_specs=[smem, smem, vmem, pl.BlockSpec(memory_space=pl.ANY), vmem],
+        in_specs=[smem, smem, smem, smem, vmem, pl.BlockSpec(memory_space=pl.ANY), vmem, vmem],
         out_specs=(vmem, vmem, vmem),
         scratch_shapes=[pltpu.VMEM((row_blocks, tok_count, tile), jnp.float32),
                         pltpu.VMEM((2, per_block * tile, tile), jnp.bfloat16),
@@ -83,7 +92,7 @@
                         pltpu.SemaphoreType.DMA(())],
         compiler_params=pltpu.CompilerParams(vmem_limit_bytes=100 * 1024 * 1024),
         interpret=interpret,
-    )(rows, slots, tok_bm, store, hgrad)
+    )(rows, slots, near, far, tok_bm, store, rest, hgrad)
 
 
 def body(tokens, hidden_grad, gate_tiles, up_tiles, tile_rows, tile_owner):
@@ -108,8 +117,23 @@
         axis=0,
     )
     local_pair = jnp.stack([gate_tiles[0], up_tiles[0]], axis=1)
-    store = lax.all_gather(local_pair, "dp", axis=0, tiled=True)
-    hidden, tpart_bm, grads_t = swiglu_local(row_flat, slot_stack, tok_bm, store, hidden_grad)
+    owner_count = lax.axis_size("dp")
+    near_count = capacity - capacity // 4
+    far_count = capacity - near_count
+    store = lax.all_gather(local_pair[:near_count], "dp", axis=0, tiled=True)
+    far_copies = jnp.broadcast_to(
+        local_pair[near_count:][None], (owner_count,) + local_pair[near_count:].shape
+    )
+    rest = lax.all_to_all(far_copies, "dp", 0, 0, tiled=True).reshape(
+        (owner_count * far_count,) + local_pair.shape[1:]
+    )
+    slot_owner = slot_stack // capacity
+    slot_rank = slot_stack % capacity
+    near = slot_owner * near_count + jnp.minimum(slot_rank, near_count - 1)
+    far = jnp.where(slot_rank >= near_count, slot_owner * far_count + slot_rank - near_count, -1)
+    hidden, tpart_bm, grads_t = swiglu_local(
+        row_flat, slot_stack, near, far, tok_bm, store, rest, hidden_grad
+    )
     token_part = tpart_bm.transpose(1, 0, 2).reshape(tok_count, model_width)
     part_rows = token_part.reshape(tensor_count, tok_count // tensor_count, model_width)
     part_recv = lax.all_to_all(part_rows, "tensor", 0, 0, tiled=True)

time: 207 us -> 263 us (1.27)
  waiting for transfers between devices: 112 us -> 152 us
  starting transfers between devices: 7.68 us -> 16.4 us
  Pallas kernels: 20.2 us -> 24.7 us
    all_to_all x0 -> x1, waiting for transfers between devices: none -> 81.6 us  [body(): lax.all_to_all(far_copies, 'dp', 0, 0, tiled=True)]
    all_gather x1, waiting for transfers between devices: 44.4 us -> 0.01 us  [body(): store = lax.all_gather(local_pair[:near_count], 'dp', axis=0, tiled=True)]
    all_to_all x0 -> x1, starting transfers between devices: none -> 8.75 us  [body(): lax.all_to_all(far_copies, 'dp', 0, 0, tiled=True)]
    pallas_call x1, Pallas kernels: 20.2 us -> 24.7 us  [swiglu_local(): pl.pallas_call(_swiglu_kernel, out_shape=out_shape, in_specs=[smem, smem,...]
  transfers between devices with their start and end apart: 3 -> 4, of which waited for: 3 -> 3; matrix products, arithmetic and copies ran while one was open for 6% -> 6% of each run, Pallas kernels for 0% -> 0%
where the time goes in v8:
time: 263 us; the launch traced here: 262 us
  waiting for transfers between devices  152 us (58%)
  blocking collectives  34.4 us (13%)
  Pallas kernels  24.7 us (9%)
  local copies, waits for them, and re-layouts  16.6 us (6%)
  starting transfers between devices  16.4 us (6%)
  between operations  14.1 us (5%)
  other arithmetic  4.58 us (2%)
    all_to_all x1, waiting for transfers between devices, body(): lax.all_to_all(far_copies, 'dp', 0, 0, tiled=True)  81.6 us
    reduce_scatter x1, waiting for transfers between devices, body(): lax.psum_scatter(grads_t, 'dp', scatter_dimension=0, tiled=True)  42.8 us
    all_to_all x1, blocking collectives, body(): part_recv = lax.all_to_all(part_rows, 'tensor', 0, 0, tiled=True)  34.4 us
    all_to_all x1, waiting for transfers between devices, body(): lax.all_to_all(tok_copies, 'tensor', 0, 0, tiled=True)  27.1 us
    pallas_call x1, Pallas kernels, swiglu_local(): pl.pallas_call(_swiglu_kernel, out_shape=out_shape, in_specs=[smem, smem,...  24.7 us
    all_to_all x1, starting transfers between devices, body(): lax.all_to_all(far_copies, 'dp', 0, 0, tiled=True)  8.75 us
    all_to_all x1, starting transfers between devices, body(): lax.all_to_all(tok_copies, 'tensor', 0, 0, tiled=True)  7.61 us
  transfers between devices with their start and end apart: 4, of which 3 were waited for; matrix products, arithmetic and copies ran while one was open for 6% of the time, Pallas kernels for 0%

profile of v8, /device:TPU:2, one launch (start us, length us, event | category | flops | bytes accessed | tf_op | source)
XLA Modules:
  0.0 262.5 jit_solution(14526199944221471955)
XLA Ops:
  7.2 2.0 fusion
  9.3 1.6 broadcast_in_dim.5
  10.8 7.6 %all-to-all-start = ((bf16[16,8,8192]{2,1,0:T(8,128)(2,1)}), bf16[16,8,8192]{2,1,0:T(8,128)(2,1)S(1)}, u32[]{:S(2)}, u32[]{:S(2)}) async-start(bf16[16,8,8192]{2,1,0:T(8,128)(2,1)} %broadcast_in_dim.5), calls=%async_computation | async-start | bytes 4194304 | tf_op jit(solution)/shard_map/all_to_all | solution.py:103
  18.5 27.1 %all-to-all-done = bf16[16,8,8192]{2,1,0:T(8,128)(2,1)S(1)} async-done(((bf16[16,8,8192]{2,1,0:T(8,128)(2,1)}), bf16[16,8,8192]{2,1,0:T(8,128)(2,1)S(1)}, u32[]{:S(2)}, u32[]{:S(2)}) %all-to-all-start) | async-done | bytes 2097184 | tf_op jit(solution)/shard_map/all_to_all | solution.py:103
  45.5 2.4 broadcast_in_dim.6
  48.0 8.7 %all-to-all-start.1 = ((bf16[16,3,2,128,128]{4,3,2,1,0:T(8,128)(2,1)}), bf16[16,3,2,128,128]{4,3,2,1,0:T(8,128)(2,1)}, u32[]{:S(2)}, u32[]{:S(2)}) async-start(bf16[16,3,2,128,128]{4,3,2,1,0:T(8,128)(2,1)} %broadcast_in_dim.6), calls=%async_computation.1 | async-start | bytes 6291456 | tf_op jit(solution)/shard_map/all_to_all | solution.py:127
  56.8 0.6 reshape.58.rows_ref
  57.5 0.1 eq.32
  57.8 0.2 convert_reduce_fusion.1
  58.0 0.2 convert_reduce_fusion
  58.2 0.6 compare_select_fusion
  58.8 0.6 minimum_add_fusion
  59.4 0.6 copy.28
  60.0 2.7 %copy.30 = bf16[128,64,128]{2,0,1:T(8,128)(2,1)} copy(bf16[128,64,128]{2,1,0:T(8,128)(2,1)S(1)} %bitcast.21) | data formatting | bytes 4194304 | tf_op jit(solution)/shard_map/reshape;reshape | solution.py:108
  62.7 81.6 %all-to-all-done.1 = bf16[16,3,2,128,128]{4,3,2,1,0:T(8,128)(2,1)} async-done(((bf16[16,3,2,128,128]{4,3,2,1,0:T(8,128)(2,1)}), bf16[16,3,2,128,128]{4,3,2,1,0:T(8,128)(2,1)}, u32[]{:S(2)}, u32[]{:S(2)}) %all-to-all-start.1) | async-done | bytes 3145760 | tf_op jit(solution)/shard_map/all_to_all | solution.py:127
  144.3 24.7 %shard_map.93 = (bf16[128,896]{1,0:T(8,128)(2,1)}, bf16[64,128,128]{2,1,0:T(8,128)(2,1)}, bf16[208,2,128,128]{3,2,1,0:T(8,128)(2,1)}) custom-call(s32[2,112]{1,0:T(2,128)} %reshape.58.rows_ref, s32[2,112]{1,0:T(2,128)} %get-tuple-element.35.slots_ref, s32[2,112]{1,0:T(2,128)} %get-tuple-element.34.near_ref, s32[2,112]{1,0:T(2,128)} %get-tuple-element.30.far_ref, ...), custom_call_target="tpu_custom_call" | custom-call | tf_op jit(solution)/shard_map/pallas_call | solution.py:83
  169.0 2.9 %copy.25 = bf16[128,64,128]{2,1,0:T(8,128)(2,1)S(1)} copy(bf16[128,64,128]{2,0,1:T(8,128)(2,1)} %bitcast.22) | data formatting | bytes 4194304 | tf_op jit(solution)/shard_map/transpose | solution.py:137
  172.0 2.3 reshape_reshape.7
  174.3 34.4 %all_to_all.15 = bf16[16,8,8192]{2,1,0:T(8,128)(2,1)S(1)} all-to-all(bf16[16,8,8192]{2,1,0:T(8,128)(2,1)} %reshape_reshape.7), channel_id=1, replica_groups=mesh['dp'=16,'tensor'=16] {'tensor'}, dimensions={0} | all-to-all | bytes 4194304 | tf_op jit(solution)/shard_map/all_to_all | solution.py:139
  208.7 1.0 reduce_sum.38
  209.7 42.8 %reduce-scatter.2.cloned.1.call-done = bf16[13,2,128,128]{3,2,1,0:T(8,128)(2,1)} async-done(((bf16[208,2,128,128]{3,2,1,0:T(8,128)(2,1)}), bf16[13,2,128,128]{3,2,1,0:T(8,128)(2,1)}) %reduce-scatter.2.cloned.1.call-update) | async-done | bytes 851984 | tf_op jit(solution)/shard_map/reduce_scatter | solution.py:141
  252.5 1.2 slice_bitcast_fusion
  253.7 1.0 copy.27
  254.7 1.0 copy.26
  (22 shorter events, 0.4 us)
Async XLA Ops:
  7.2 2.1 copy-start.2
  7.2 137.1 %all-gather.2.cloned.1.call-start = ((), (), s32[]{:S(2)}) async-start(), calls=%async_computation.4 | async-start | bytes 11141120 | tf_op jit(solution)/shard_map/all_gather | solution.py:123
  10.8 7.6 %copy-start = (bf16[1,13,128,128]{3,2,1,0:T(8,128)(2,1)S(1)}, bf16[1,13,128,128]{3,2,1,0:T(8,128)(2,1)}, u32[]{:S(2)}) copy-start(bf16[1,13,128,128]{3,2,1,0:T(8,128)(2,1)} %param.8) | copy-start | bytes 1277956
  10.8 7.6 %copy-start.1 = (bf16[1,13,128,128]{3,2,1,0:T(8,128)(2,1)S(1)}, bf16[1,13,128,128]{3,2,1,0:T(8,128)(2,1)}, u32[]{:S(2)}) copy-start(bf16[1,13,128,128]{3,2,1,0:T(8,128)(2,1)} %param.9) | copy-start | bytes 1277956
  10.8 34.7 %all-to-all-start = ((bf16[16,8,8192]{2,1,0:T(8,128)(2,1)}), bf16[16,8,8192]{2,1,0:T(8,128)(2,1)S(1)}, u32[]{:S(2)}, u32[]{:S(2)}) async-start(bf16[16,8,8192]{2,1,0:T(8,128)(2,1)} %broadcast_in_dim.5), calls=%async_computation | async-start | bytes 4194304 | tf_op jit(solution)/shard_map/all_to_all | solution.py:103
  48.0 8.8 %copy-start.3 = (s32[2,7,16]{2,0,1:T(2,128)S(1)}, s32[2,7,16]{2,0,1:T(2,128)}, u32[]{:S(2)}) copy-start(s32[2,7,16]{2,0,1:T(2,128)} %param.10) | copy-start | bytes 2692
  48.0 9.5 %copy-start.4 = (s32[2,7,16]{2,0,1:T(2,128)S(1)}, s32[2,7,16]{2,0,1:T(2,128)}, u32[]{:S(2)}) copy-start(s32[2,7,16]{2,0,1:T(2,128)} %param.11) | copy-start | bytes 2692
  48.0 96.3 %all-to-all-start.1 = ((bf16[16,3,2,128,128]{4,3,2,1,0:T(8,128)(2,1)}), bf16[16,3,2,128,128]{4,3,2,1,0:T(8,128)(2,1)}, u32[]{:S(2)}, u32[]{:S(2)}) async-start(bf16[16,3,2,128,128]{4,3,2,1,0:T(8,128)(2,1)} %broadcast_in_dim.6), calls=%async_computation.1 | async-start | bytes 6291456 | tf_op jit(solution)/shard_map/all_to_all | solution.py:127
  56.8 195.8 %reduce-scatter.2.cloned.1.call-start = ((), (), s32[]{:S(2)}) async-start(), calls=%async_computation.5 | async-start | bytes 14483456 | tf_op jit(solution)/shard_map/reduce_scatter | solution.py:141
Sparse Core Ops, SparseCore 0:
  9.8 110.3 all-gather.1
  169.2 83.3 reduce-scatter.1
